TPU v7x, 512 devices: a whole 4x8x8 slice. The times are simulated.
512 devices in a mesh: req: 128 (over y, z, core), mlp: 4 (over x).
Axes of the slice: x: 4, y: 8, z: 8, core: 2. Of those that a mesh axis runs over, the one named last changes fastest.
Arguments:
- residual: bfloat16 [32768, 2048], P('req'), may hold values from -20 to 20
- query_rows: bfloat16 [32768, 2048], P('req', 'mlp'), may hold values from -6 to 6
- value_rows: bfloat16 [32768, 2048], P('req', 'mlp'), may hold values from -6 to 6
- forget_logit: float32 [32768, 2048], P('req', 'mlp'), may hold values from 0 to 40
- slot_kind: int32 [32768], P('req'), may hold values from 0 to 2, as said below
- head_gain: float32 [2048], P('mlp'), may hold values from 0.1 to 1.9
- out_weight: bfloat16 [2048, 2048], P('mlp', 'req'), may hold values from -0.125 to 0.125
- ffn_gain: float32 [2048], replicated, may hold values from 0.1 to 1.9
- gate_weight: bfloat16 [2048, 3072], P('req', 'mlp'), may hold values from -0.125 to 0.125
- up_weight: bfloat16 [2048, 3072], P('req', 'mlp'), may hold values from -0.125 to 0.125
- down_weight: bfloat16 [3072, 2048], P('mlp', 'req'), may hold values from -0.109375 to 0.109375
Outputs:
- layer_out: bfloat16 [32768, 2048], P('req', 'mlp')
Inputs may be any that keep to these rules, and one draw needn't show every extreme that they name: `slot_kind`: slots 0 to 24575 hold one prompt: slot 0 has kind 2, the others kind 1. Every other block of 256 slots holds short requests packed from its first slot, then empty slots; a short request has at most 32 tokens, the first request of each such block exactly 32. Over all 32768 slots exactly 26624 are live.
All inputs are finite; a program needn't handle non-finite values.
Results may differ from a plain program's by a relative error of at most 0.0163.
Values may be sent and summed in bfloat16 or wider, within the bound.
No kernel may reach another device: no remote copies, remote signals or barrier semaphores. Data moves between devices by JAX's collectives and lax.ppermute only.
A program may use at most 128 MiB of HBM per device.

v0:
```python
import jax
import jax.numpy as jnp
from jax import lax
from jax.sharding import PartitionSpec as P

HEAD = 128
SPAN = 32


def carried_in(part, axis, combine, identity):
    place = lax.axis_index(axis)
    gathered = jax.tree.map(lambda a: lax.all_gather(a, axis), part)
    state = jax.tree.map(lambda a, e: jnp.zeros_like(a) + jnp.asarray(e, a.dtype), part, identity)

    def one(hop, state):
        return combine(
            state, jax.tree.map(lambda a: lax.dynamic_index_in_dim(a, hop, 0, False), gathered)
        )

    return lax.fori_loop(0, place, one, state)


def span_step(passed_state, pieces):
    query_block, key_block, value_block, g_block = pieces
    top_precision = lax.Precision.HIGHEST
    inside_block_term = jnp.cumsum(g_block, axis=0)
    between_blocks_term = jnp.einsum(
        "owu,wuj->owj",
        query_block * jnp.exp(inside_block_term),
        passed_state,
        precision=top_precision,
    )
    length = g_block.shape[0]
    causal = jnp.arange(length)[:, None] >= jnp.arange(length)[None, :]
    causal = causal[:, :, None, None]
    gap_log = jnp.where(causal, inside_block_term[:, None] - inside_block_term[None, :], 0.0)
    decay_pairs = jnp.where(causal, jnp.exp(gap_log), 0.0)
    scores = jnp.einsum(
        "tnk,tsnk->tsn", query_block, decay_pairs * key_block[None], precision=top_precision
    )
    intra_part = jnp.einsum("tsn,snv->tnv", scores, value_block, precision=top_precision)
    final_decay_sum = inside_block_term[-1]
    updated_state = jnp.exp(final_decay_sum)[:, :, None] * passed_state + jnp.einsum(
        "weq,wel->eql",
        key_block * jnp.exp(final_decay_sum[None] - inside_block_term),
        value_block,
        precision=top_precision,
    )
    return (updated_state, between_blocks_term + intra_part)


def compose(earlier, later):
    return (
        earlier[0] * later[0],
        later[0][:, :, None] * earlier[1] + later[1],
        earlier[2] + later[2],
    )


def on_device(
    residual,
    query_rows,
    value_rows,
    forget_logit,
    slot_kind,
    head_gain,
    out_weight,
    ffn_gain,
    gate_weight,
    up_weight,
    down_weight,
):
    slot_total = residual.shape[0]
    quarter = query_rows.shape[1]
    heads_here = quarter // HEAD
    live_mask = slot_kind > 0
    first_mask = slot_kind == 2
    log_forget = jnp.where(
        first_mask[:, None],
        -80.0,
        jnp.where(live_mask[:, None], -jax.nn.softplus(-forget_logit), 0.0),
    )
    key_gate = jnp.where(live_mask[:, None], jax.nn.sigmoid(-forget_logit), 0.0)
    shape4 = (slot_total // SPAN, SPAN, heads_here, HEAD)
    q_all = query_rows.astype(jnp.float32).reshape(shape4)
    v_all = value_rows.astype(jnp.float32).reshape(shape4)
    k_all = key_gate.reshape(shape4)
    g_all = log_forget.reshape(shape4)
    zero_state = jnp.zeros((heads_here, HEAD, HEAD), jnp.float32)
    decay_whole = jnp.exp(jnp.sum(log_forget, axis=0)).reshape(heads_here, HEAD)
    live_count = jnp.sum(live_mask.astype(jnp.float32))
    neutral = (jnp.ones_like(decay_whole), jnp.zeros_like(zero_state), jnp.zeros((), jnp.float32))
    end_state, local_out = lax.scan(span_step, zero_state, (q_all, k_all, v_all, g_all))
    leading_decay = carried_in((decay_whole, end_state, live_count), "req", compose, neutral)
    within_all = jnp.cumsum(g_all, axis=1)
    block_total = within_all[:, -1]
    before_block = jnp.cumsum(block_total, axis=0) - block_total
    query_damped = q_all * jnp.exp(within_all + before_block[:, None])
    heads_out = local_out + jnp.einsum(
        "mosf,sfl->mosl", query_damped, leading_decay[1], precision=lax.Precision.HIGHEST
    )
    heads_out = heads_out.reshape(slot_total, heads_here, HEAD)
    mean_sq = jnp.mean(heads_out * heads_out, axis=-1, keepdims=True)
    head_normed = (
        heads_out / jnp.sqrt(mean_sq + 1e-06) * head_gain.reshape(heads_here, HEAD)
    ).astype(jnp.bfloat16)
    head_normed = head_normed.reshape(slot_total, quarter)
    partial_rows = jnp.dot(
        head_normed,
        lax.all_gather(out_weight, "req", axis=1, tiled=True),
        preferred_element_type=jnp.float32,
    )
    mixed_sum = lax.psum(partial_rows.astype(jnp.bfloat16), "mlp").astype(jnp.float32)
    stream = (residual.astype(jnp.float32) + mixed_sum).astype(jnp.bfloat16)
    my_cols = lax.axis_index("mlp") * quarter
    rows_f = stream.astype(jnp.float32)
    ffn_in = (
        rows_f / jnp.sqrt(jnp.mean(rows_f * rows_f, axis=-1, keepdims=True) + 1e-05) * ffn_gain
    ).astype(jnp.bfloat16)
    gate_acc = jnp.dot(
        ffn_in,
        lax.all_gather(gate_weight, "req", axis=0, tiled=True),
        preferred_element_type=jnp.float32,
    )
    up_acc = jnp.dot(
        ffn_in,
        lax.all_gather(up_weight, "req", axis=0, tiled=True),
        preferred_element_type=jnp.float32,
    )
    hidden = (jax.nn.silu(gate_acc) * up_acc).astype(jnp.bfloat16)
    terms = jnp.dot(
        hidden,
        lax.all_gather(down_weight, "req", axis=1, tiled=True),
        preferred_element_type=jnp.float32,
    )
    ffn_out = lax.psum_scatter(
        terms.astype(jnp.bfloat16), "mlp", scatter_dimension=1, tiled=True
    ).astype(jnp.float32)
    own_cols = lax.dynamic_slice_in_dim(stream, my_cols, quarter, 1).astype(jnp.float32)
    result = (own_cols + ffn_out).astype(jnp.bfloat16)
    layer_out = jnp.where(live_mask[:, None], result, jnp.zeros_like(result))
    return layer_out


def solution(mesh):
    return jax.shard_map(
        on_device,
        mesh=mesh,
        in_specs=(
            P("req", None),
            P("req", "mlp"),
            P("req", "mlp"),
            P("req", "mlp"),
            P("req"),
            P("mlp"),
            P("mlp", "req"),
            P(),
            P("req", "mlp"),
            P("req", "mlp"),
            P("mlp", "req"),
        ),
        out_specs=P("req", "mlp"),
        check_vma=False,
    )
```

profile of v0, /device:TPU:40, one launch (start us, length us, event | category | flops | bytes accessed | tf_op | source)
XLA Modules:
  0.0 705.8 jit_solution(7420464183667757412)
XLA Ops:
  9.6 50.4 %while.27 = (s32[]{:T(128)}, f32[4,128,128]{2,1,0:T(8,128)S(1)}, f32[8,32,4,128]{3,1,0,2:T(8,128)S(1)}, f32[8,32,4,128]{3,2,1,0:T(4,128)S(1)}, f32[8,32,4,128]{3...) while((s32[]{:T(128)}, f32[4,128,128]{2,1,0:T(8,128)S(1)}, ...), condition=%wide.region_2.3_spmd.clone, body=%wide.region_0.2_spmd.clone.sunk | while | flops 65848320 | bytes 6453368 | solution.py:93
  9.7 1.6 select_multiply_fusion.2
  11.3 3.3 fusion.68
  16.0 1.6 select_multiply_fusion.2
  17.6 3.3 fusion.68
  23.9 3.3 fusion.68
  30.2 3.3 fusion.68
  36.5 3.3 fusion.68
  42.8 3.3 fusion.68
  49.1 3.3 fusion.68
  55.4 3.3 fusion.68
  62.4 55.8 %all_gather.23 = f32[128,4,128]{2,1,0:T(4,128)S(1)} all-gather(f32[1,4,128]{2,1,0:T(4,128)S(1)} %exponential_bitcast_fusion), channel_id=1, replica_groups=mesh['req'=128,'mlp'=4] {'req'}, dimensions={0}, use_global_device_ids=true | all-gather | bytes 264192 | tf_op jit(solution)/shard_map/all_gather | solution.py:12
  118.2 88.0 %all-gather.15.cloned.1.call-done = f32[512,128,128]{2,1,0:T(8,128)} async-done(((f32[4,128,128]{2,1,0:T(8,128)}), f32[512,128,128]{2,1,0:T(8,128)}) %all-gather.15.cloned.1.call-update) | async-done | bytes 33554448 | tf_op jit(solution)/shard_map/all_gather | solution.py:12
  206.3 93.1 %while.26 = (s32[]{:T(128)}, f32[4,128,128]{2,1,0:T(8,128)S(1)}, s32[]{:T(128)}, f32[128,4,128]{2,1,0:T(4,128)S(1)}, f32[128,4,128,128]{3,2,1,0:T(8,128)}, /*index=5*/s32[]{:T(128)}, s32[]{:T(128)}, s32[]{:T(128)}) while((s32[]{:T(128)}, f32[4,128,128]{2,1,0:T(8,128)S(1)}, s32[]{:T(128)}, f32[128,4,128]{2,1,0:T(4,128)S(1)}, ...), condition=%wide.region_5.6_spmd, body=%wide.region_4.5_spmd.sunk | while | flops 131077 | bytes 792703 | solution.py:20
  301.2 3.4 convolution_convert_fusion
  306.6 103.3 %all-reduce.2.cloned.1.call-done = bf16[256,2048]{1,0:T(8,128)(2,1)} async-done(((bf16[256,2048]{1,0:T(8,128)(2,1)}), bf16[256,2048]{1,0:T(8,128)(2,1)}) %all-reduce.2.cloned.1.call-update) | async-done | bytes 1048592 | tf_op jit(solution)/shard_map/psum | solution.py:113
  409.9 1.7 fusion.18
  411.6 84.6 %all-gather.9.cloned.1.call-done = bf16[2048,768]{1,0:T(8,128)(2,1)} async-done(((bf16[16,768]{1,0:T(8,128)(2,1)}), bf16[2048,768]{1,0:T(8,128)(2,1)}) %all-gather.9.cloned.1.call-update) | async-done | bytes 3145744 | tf_op jit(solution)/shard_map/all_gather | solution.py:122
  496.2 2.9 fusion.36
  499.1 80.7 %all-gather.11.cloned.1.call-done = bf16[2048,768]{1,0:T(8,128)(2,1)} async-done(((bf16[16,768]{1,0:T(8,128)(2,1)}), bf16[2048,768]{1,0:T(8,128)(2,1)}) %all-gather.11.cloned.1.call-update) | async-done | bytes 3145744 | tf_op jit(solution)/shard_map/all_gather | solution.py:127
  579.9 83.7 %all-gather.13.cloned.1.call-done = bf16[768,2048]{0,1:T(8,128)(2,1)} async-done(((bf16[768,16]{0,1:T(8,128)(2,1)}), bf16[768,2048]{0,1:T(8,128)(2,1)}) %all-gather.13.cloned.1.call-update) | async-done | bytes 3145744 | tf_op jit(solution)/shard_map/all_gather | solution.py:133
  663.6 6.1 convolution_convert_fusion.1
  669.7 27.6 %reduce-scatter.2.cloned.1.call-done = bf16[256,512]{1,0:T(8,128)(2,1)} async-done(((bf16[256,2048]{1,0:T(8,128)(2,1)}), bf16[256,512]{1,0:T(8,128)(2,1)}) %reduce-scatter.2.cloned.1.call-update) | async-done | bytes 262160 | tf_op jit(solution)/shard_map/reduce_scatter | solution.py:136
  697.2 1.8 fusion.30
  (288 shorter events, 118.9 us)
Async XLA Ops:
  6.5 2.5 copy-start.2
  6.5 199.8 %all-gather.15.cloned.1.call-start = ((), (), s32[]{:S(2)}) async-start(), calls=%async_computation.7 | async-start | bytes 33816576 | tf_op jit(solution)/shard_map/all_gather | solution.py:12
  7.3 2.1 copy-start.3
  60.0 0.7 copy-start
  60.7 240.1 %all-gather.7.cloned.1.call-start = ((), (), s32[]{:S(2)}) async-start(), calls=%async_computation.1 | async-start | bytes 2113536 | tf_op jit(solution)/shard_map/all_gather | solution.py:110
  61.5 348.4 %all-reduce.2.cloned.1.call-start = ((), (), s32[]{:S(2)}) async-start(), calls=%async_computation.2 | async-start | bytes 2097152 | tf_op jit(solution)/shard_map/psum | solution.py:113
  299.5 1.7 copy-start.5
  301.2 108.7 %copy-start.1 = (bf16[256,2048]{1,0:T(8,128)(2,1)S(1)}, bf16[256,2048]{1,0:T(8,128)(2,1)}, u32[]{:S(2)}) copy-start(bf16[256,2048]{1,0:T(8,128)(2,1)} %param.15) | copy-start | bytes 3145732
  304.6 191.6 %copy-start.4 = (f32[2048]{0:T(1024)S(1)}, f32[2048]{0:T(1024)}, u32[]{:S(2)}) copy-start(f32[2048]{0:T(1024)} %param.22) | copy-start | bytes 24580
  304.6 191.6 %all-gather.9.cloned.1.call-start = ((), (), s32[]{:S(2)}) async-start(), calls=%async_computation.3 | async-start | bytes 3170304 | tf_op jit(solution)/shard_map/all_gather | solution.py:122
  305.2 274.7 %all-gather.11.cloned.1.call-start = ((), (), s32[]{:S(2)}) async-start(), calls=%async_computation.4 | async-start | bytes 3170304 | tf_op jit(solution)/shard_map/all_gather | solution.py:127
  305.8 357.8 %all-gather.13.cloned.1.call-start = ((), (), s32[]{:S(2)}) async-start(), calls=%async_computation.5 | async-start | bytes 3170304 | tf_op jit(solution)/shard_map/all_gather | solution.py:133
  306.3 390.9 %reduce-scatter.2.cloned.1.call-start = ((), (), s32[]{:S(2)}) async-start(), calls=%async_computation.6 | async-start | bytes 1310720 | tf_op jit(solution)/shard_map/reduce_scatter | solution.py:136
Sparse Core Ops, SparseCore 0:
  60.8 145.4 all-gather.14
  209.4 79.7 all-gather.6
  304.7 105.0 all-reduce.1
  412.8 83.2 all-gather.8
  499.1 80.6 all-gather.10
  582.8 80.6 all-gather.12
  669.8 27.3 reduce-scatter.1
where the time goes:
time: 710 us; the launch traced here: 706 us
  waiting for transfers between devices  470 us (66%)
  other arithmetic  110 us (15%)
  blocking collectives  55.8 us (8%)
  matrix products  49.3 us (7%)
  between operations  13.7 us (2%)
    psum x1, waiting for transfers between devices, on_device(): lax.psum(partial_rows.astype(jnp.bfloat16), 'mlp').astype(jnp.float32)  103 us
    add x80, other arithmetic, compose(): later[0][:, :, None] * earlier[1] + later[1]  89.4 us
    all_gather x1, waiting for transfers between devices, carried_in(): gathered = jax.tree.map(lambda a: lax.all_gather(a, axis), part)  88 us
    all_gather x1, waiting for transfers between devices, on_device(): lax.all_gather(gate_weight, 'req', axis=0, tiled=True)  84.6 us
    all_gather x1, waiting for transfers between devices, on_device(): lax.all_gather(down_weight, 'req', axis=1, tiled=True)  83.7 us
    all_gather x1, waiting for transfers between devices, on_device(): lax.all_gather(up_weight, 'req', axis=0, tiled=True)  80.7 us
    all_gather x1, blocking collectives, carried_in(): gathered = jax.tree.map(lambda a: lax.all_gather(a, axis), part)  55.8 us
    reduce_scatter x1, waiting for transfers between devices, on_device(): lax.psum_scatter(terms.astype(jnp.bfloat16), 'mlp', scatter_dimension=1,...  27.6 us
  transfers between devices with their start and end apart: 7, of which 6 were waited for; matrix products, arithmetic and copies ran while one was open for 14% of the time, Pallas kernels for 0%

commit v1 on v0

v1 whole, which is shorter than its diff:
```python
import jax
import jax.numpy as jnp
from jax import lax
from jax.sharding import Mesh, PartitionSpec as P

HEAD = 128
SPAN = 32
TOP = lax.Precision.HIGHEST
REQ = ("rp", "rc")


def span_step(passed_state, pieces):
    query_block, key_block, value_block, g_block = pieces
    inside_block_term = jnp.cumsum(g_block, axis=0)
    between_blocks_term = jnp.einsum(
        "owu,wuj->owj",
        query_block * jnp.exp(inside_block_term),
        passed_state,
        precision=TOP,
    )
    length = g_block.shape[0]
    causal = jnp.arange(length)[:, None] >= jnp.arange(length)[None, :]
    causal = causal[:, :, None, None]
    gap_log = jnp.where(causal, inside_block_term[:, None] - inside_block_term[None, :], 0.0)
    decay_pairs = jnp.where(causal, jnp.exp(gap_log), 0.0)
    scores = jnp.einsum("tnk,tsnk->tsn", query_block, decay_pairs * key_block[None], precision=TOP)
    intra_part = jnp.einsum("tsn,snv->tnv", scores, value_block, precision=TOP)
    final_decay_sum = inside_block_term[-1]
    updated_state = jnp.exp(final_decay_sum)[:, :, None] * passed_state + jnp.einsum(
        "weq,wel->eql",
        key_block * jnp.exp(final_decay_sum[None] - inside_block_term),
        value_block,
        precision=TOP,
    )
    return (updated_state, between_blocks_term + intra_part)


def compose(earlier, later):
    return (earlier[0] * later[0], later[0][:, :, None] * earlier[1] + later[1])


def carried_in(decay, state, count):
    place = lax.axis_index(REQ)
    ones = jnp.ones_like(decay)
    decay, state = lax.ppermute((decay, state), REQ, [(i, i + 1) for i in range(count - 1)])
    decay = jnp.where(place == 0, ones, decay)
    hop = 1
    while hop < count:
        got = lax.ppermute((decay, state), REQ, [(i, i + hop) for i in range(count - hop)])
        joined = compose(got, (decay, state))
        take = place >= hop
        decay = jnp.where(take, joined[0], decay)
        state = jnp.where(take, joined[1], state)
        hop *= 2
    return state


def mlp_sum(parts, n_mlp):
    rows, width = parts.shape
    blocks = parts.reshape(rows, n_mlp, width // n_mlp).transpose(1, 0, 2)
    got = lax.all_to_all(blocks, "mlp", 0, 0)
    return jnp.sum(got.astype(jnp.float32), axis=0)


def mlp_gather(cols, n_mlp):
    rows, width = cols.shape
    sent = jnp.broadcast_to(cols[None], (n_mlp, rows, width))
    got = lax.all_to_all(sent, "mlp", 0, 0)
    return got.transpose(1, 0, 2).reshape(rows, n_mlp * width)


def on_device(
    residual,
    query_rows,
    value_rows,
    forget_logit,
    slot_kind,
    head_gain,
    out_weight,
    ffn_gain,
    gate_weight,
    up_weight,
    down_weight,
    *,
    n_pairs,
    n_mlp,
):
    slot_total = residual.shape[0]
    quarter = query_rows.shape[1]
    heads_here = quarter // HEAD
    hidden_here = gate_weight.shape[1]

    packed = jnp.concatenate([gate_weight, up_weight, out_weight.T, down_weight.T], axis=1)
    over_chips = lax.all_gather(packed, "rp", axis=0)
    over_cores = lax.all_gather(over_chips, "rc", axis=0)
    rows_each = packed.shape[0]
    full = over_cores.transpose(1, 0, 2, 3).reshape(2 * n_pairs * rows_each, packed.shape[1])
    gate_full = full[:, :hidden_here]
    up_full = full[:, hidden_here:2 * hidden_here]
    out_t = full[:, 2 * hidden_here:2 * hidden_here + quarter]
    down_t = full[:, 2 * hidden_here + quarter:]

    live_mask = slot_kind > 0
    first_mask = slot_kind == 2
    log_forget = jnp.where(
        first_mask[:, None],
        -80.0,
        jnp.where(live_mask[:, None], -jax.nn.softplus(-forget_logit), 0.0),
    )
    key_gate = jnp.where(live_mask[:, None], jax.nn.sigmoid(-forget_logit), 0.0)
    shape3 = (slot_total, heads_here, HEAD)
    q3 = query_rows.astype(jnp.float32).reshape(shape3)
    v3 = value_rows.astype(jnp.float32).reshape(shape3)
    k3 = key_gate.reshape(shape3)
    g3 = log_forget.reshape(shape3)

    running = jnp.cumsum(g3, axis=0)
    total = running[-1]
    end_state = jnp.einsum(
        "thk,thv->hkv", k3 * jnp.exp(total[None] - running), v3, precision=TOP
    )
    state_in = carried_in(jnp.exp(total), end_state, 2 * n_pairs)

    shape4 = (slot_total // SPAN, SPAN, heads_here, HEAD)
    zero_state = jnp.zeros((heads_here, HEAD, HEAD), jnp.float32)
    _, local_out = lax.scan(
        span_step,
        zero_state,
        (q3.reshape(shape4), k3.reshape(shape4), v3.reshape(shape4), g3.reshape(shape4)),
    )
    heads_out = local_out.reshape(shape3) + jnp.einsum(
        "thk,hkv->thv", q3 * jnp.exp(running), state_in, precision=TOP
    )
    mean_sq = jnp.mean(heads_out * heads_out, axis=-1, keepdims=True)
    head_normed = (
        heads_out / jnp.sqrt(mean_sq + 1e-06) * head_gain.reshape(heads_here, HEAD)
    ).astype(jnp.bfloat16)
    head_normed = head_normed.reshape(slot_total, quarter)
    partial_rows = lax.dot_general(
        head_normed, out_t, (((1,), (1,)), ((), ())), preferred_element_type=jnp.float32
    ).astype(jnp.bfloat16)
    mixed_cols = mlp_sum(partial_rows, n_mlp)
    my_cols = lax.axis_index("mlp") * quarter
    own_res = lax.dynamic_slice_in_dim(residual, my_cols, quarter, 1).astype(jnp.float32)
    stream_cols = (own_res + mixed_cols).astype(jnp.bfloat16)
    stream = mlp_gather(stream_cols, n_mlp)

    rows_f = stream.astype(jnp.float32)
    ffn_in = (
        rows_f / jnp.sqrt(jnp.mean(rows_f * rows_f, axis=-1, keepdims=True) + 1e-05) * ffn_gain
    ).astype(jnp.bfloat16)
    gate_acc = jnp.dot(ffn_in, gate_full, preferred_element_type=jnp.float32)
    up_acc = jnp.dot(ffn_in, up_full, preferred_element_type=jnp.float32)
    hidden = (jax.nn.silu(gate_acc) * up_acc).astype(jnp.bfloat16)
    terms = lax.dot_general(
        hidden, down_t, (((1,), (1,)), ((), ())), preferred_element_type=jnp.float32
    ).astype(jnp.bfloat16)
    ffn_out = mlp_sum(terms, n_mlp)
    result = (stream_cols.astype(jnp.float32) + ffn_out).astype(jnp.bfloat16)
    return jnp.where(live_mask[:, None], result, jnp.zeros_like(result))


def solution(mesh):
    n_req = mesh.shape["req"]
    n_mlp = mesh.shape["mlp"]
    n_pairs = n_req // 2
    split = Mesh(mesh.devices.reshape(n_pairs, 2, n_mlp), ("rp", "rc", "mlp"))

    def body(*args):
        return on_device(*args, n_pairs=n_pairs, n_mlp=n_mlp)

    return jax.shard_map(
        body,
        mesh=split,
        in_specs=(
            P(REQ, None),
            P(REQ, "mlp"),
            P(REQ, "mlp"),
            P(REQ, "mlp"),
            P(REQ),
            P("mlp"),
            P("mlp", REQ),
            P(),
            P(REQ, "mlp"),
            P(REQ, "mlp"),
            P("mlp", REQ),
        ),
        out_specs=P(REQ, "mlp"),
        check_vma=False,
    )
```

time: 710 us -> 277 us (0.39)
  the two profiles are of different devices: /device:TPU:40 before, /device:TPU:72 now
where the time goes in v1:
time: 277 us; the launch traced here: 275 us
  starting transfers between devices  74.4 us (27%)
  waiting for transfers between devices  58.8 us (21%)
  matrix products  52.3 us (19%)
  other arithmetic  29.8 us (11%)
  blocking collectives  28.6 us (10%)
  local copies, waits for them, and re-layouts  17.4 us (6%)
  between operations  13.9 us (5%)
    ppermute x13, starting transfers between devices, carried_in(): lax.ppermute((decay, state), REQ, [(i, i + hop) for i in range(count - ho...  63.7 us
    ppermute x13, waiting for transfers between devices, carried_in(): lax.ppermute((decay, state), REQ, [(i, i + hop) for i in range(count - ho...  38 us
    dot_general x8, matrix products, span_step(): jnp.einsum('tnk,tsnk->tsn', query_block, decay_pairs * key_block[None], p...  26.8 us
    all_to_all x1, blocking collectives, mlp_gather(): got = lax.all_to_all(sent, 'mlp', 0, 0)  14.9 us
    all_to_all x1, blocking collectives, mlp_sum(): got = lax.all_to_all(blocks, 'mlp', 0, 0)  13.7 us
    all_to_all x1, waiting for transfers between devices, mlp_sum(): got = lax.all_to_all(blocks, 'mlp', 0, 0)  13.6 us
    mul x8, other arithmetic, span_step(): decay_pairs * key_block[None]  12.5 us
    mul x8, other arithmetic, span_step(): query_block * jnp.exp(inside_block_term)  7.27 us
  transfers between devices with their start and end apart: 18, of which 9 were waited for; matrix products, arithmetic and copies ran while one was open for 27% of the time, Pallas kernels for 0%

profile of v1, /device:TPU:72, one launch (start us, length us, event | category | flops | bytes accessed | tf_op | source)
XLA Modules:
  0.0 275.5 jit_solution(11766271191527473415)
XLA Ops:
  14.6 5.8 %collective-permute-done.7 = f32[4,128,128]{2,1,0:T(8,128)S(1)} collective-permute-done((f32[4,128,128]{2,1,0:T(8,128)S(1)}, f32[4,128,128]{2,1,0:T(8,128)S(1)}, u32[]{:S(2)}, u32[]{:S(2)}) %collective-permute-start.7) | collective-permute-done | bytes 262176 | tf_op jit(solution)/shard_map/ppermute | solution.py:45
  22.3 4.4 %collective-permute-start = (f32[4,128]{1,0:T(4,128)S(1)}, f32[4,128]{1,0:T(4,128)S(1)}, u32[]{:S(2)}, u32[]{:S(2)}) collective-permute-start(f32[4,128]{1,0:T(4,128)S(1)} %exp.38), channel_id=1, source_target_pairs={{0,4},{4,8},{8,12},{12,16},{16,20},{20,24},{24,28},{28,32},{32,36}... | collective-permute-start | bytes 6152 | tf_op jit(solution)/shard_map/ppermute | solution.py:45
  28.2 4.3 %collective-permute-start.9 = (f32[4,128,128]{2,1,0:T(8,128)S(1)}, f32[4,128,128]{2,1,0:T(8,128)S(1)}, u32[]{:S(2)}, u32[]{:S(2)}) collective-permute-start(f32[4,128,128]{2,1,0:T(8,128)S(1)} %add_select_fusion.6), channel_id=1, source_target_pairs={{0,8},{4,12},{8,16},{12,20},{16,24},{20,28},{24,32},{28,36},{32,40... | collective-permute-start | bytes 786440 | tf_op jit(solution)/shard_map/ppermute | solution.py:49
  37.8 6.0 %collective-permute-done.9 = f32[4,128,128]{2,1,0:T(8,128)S(1)} collective-permute-done((f32[4,128,128]{2,1,0:T(8,128)S(1)}, f32[4,128,128]{2,1,0:T(8,128)S(1)}, u32[]{:S(2)}, u32[]{:S(2)}) %collective-permute-start.9) | collective-permute-done | bytes 262176 | tf_op jit(solution)/shard_map/ppermute | solution.py:49
  44.0 4.4 %collective-permute-start.10 = (f32[4,128,128]{2,1,0:T(8,128)S(1)}, f32[4,128,128]{2,1,0:T(8,128)S(1)}, u32[]{:S(2)}, u32[]{:S(2)}) collective-permute-start(f32[4,128,128]{2,1,0:T(8,128)S(1)} %add_select_fusion.5), channel_id=1, source_target_pairs={{0,16},{4,20},{8,24},{12,28},{16,32},{20,36},{24,40},{28,44},{32,4... | collective-permute-start | bytes 786440 | tf_op jit(solution)/shard_map/ppermute | solution.py:49
  52.7 7.6 %collective-permute-done.2 = f32[4,128]{1,0:T(4,128)S(1)} collective-permute-done((f32[4,128]{1,0:T(4,128)S(1)}, f32[4,128]{1,0:T(4,128)S(1)}, u32[]{:S(2)}, u32[]{:S(2)}) %collective-permute-start.2) | collective-permute-done | bytes 2080 | tf_op jit(solution)/shard_map/ppermute | solution.py:49
  60.5 6.1 %collective-permute-start.11 = (f32[4,128,128]{2,1,0:T(8,128)S(1)}, f32[4,128,128]{2,1,0:T(8,128)S(1)}, u32[]{:S(2)}, u32[]{:S(2)}) collective-permute-start(f32[4,128,128]{2,1,0:T(8,128)S(1)} %add_select_fusion.4), channel_id=1, source_target_pairs={{0,32},{4,36},{8,40},{12,44},{16,48},{20,52},{24,56},{28,60},{32,6... | collective-permute-start | bytes 786440 | tf_op jit(solution)/shard_map/ppermute | solution.py:49
  70.1 8.4 %collective-permute-done.3 = f32[4,128]{1,0:T(4,128)S(1)} collective-permute-done((f32[4,128]{1,0:T(4,128)S(1)}, f32[4,128]{1,0:T(4,128)S(1)}, u32[]{:S(2)}, u32[]{:S(2)}) %collective-permute-start.3) | collective-permute-done | bytes 2080 | tf_op jit(solution)/shard_map/ppermute | solution.py:49
  78.7 5.8 %collective-permute-start.12 = (f32[4,128,128]{2,1,0:T(8,128)S(1)}, f32[4,128,128]{2,1,0:T(8,128)S(1)}, u32[]{:S(2)}, u32[]{:S(2)}) collective-permute-start(f32[4,128,128]{2,1,0:T(8,128)S(1)} %add_select_fusion.3), channel_id=1, source_target_pairs={{0,64},{4,68},{8,72},{12,76},{16,80},{20,84},{24,88},{28,92},{32,9... | collective-permute-start | bytes 786440 | tf_op jit(solution)/shard_map/ppermute | solution.py:49
  84.5 8.3 %collective-permute-start.4 = (f32[4,128]{1,0:T(4,128)S(1)}, f32[4,128]{1,0:T(4,128)S(1)}, u32[]{:S(2)}, u32[]{:S(2)}) collective-permute-start(f32[4,128]{1,0:T(4,128)S(1)} %multiply_select_fusion.3), channel_id=1, source_target_pairs={{0,32},{4,36},{8,40},{12,44},{16,48},{20,52},{24,56},{28,60},{32,6... | collective-permute-start | bytes 6152 | tf_op jit(solution)/shard_map/ppermute | solution.py:49
  92.8 5.7 %collective-permute-done.4 = f32[4,128]{1,0:T(4,128)S(1)} collective-permute-done((f32[4,128]{1,0:T(4,128)S(1)}, f32[4,128]{1,0:T(4,128)S(1)}, u32[]{:S(2)}, u32[]{:S(2)}) %collective-permute-start.4) | collective-permute-done | bytes 2080 | tf_op jit(solution)/shard_map/ppermute | solution.py:49
  99.4 8.3 %collective-permute-start.13 = (f32[4,128,128]{2,1,0:T(8,128)}, f32[4,128,128]{2,1,0:T(8,128)}, u32[]{:S(2)}, u32[]{:S(2)}) collective-permute-start(f32[4,128,128]{2,1,0:T(8,128)} %add_select_fusion.2), channel_id=1, source_target_pairs={{0,128},{4,132},{8,136},{12,140},{16,144},{20,148},{24,152},{28,15... | collective-permute-start | bytes 786440 | tf_op jit(solution)/shard_map/ppermute | solution.py:49
  107.8 4.4 %collective-permute-start.5 = (f32[4,128]{1,0:T(4,128)S(1)}, f32[4,128]{1,0:T(4,128)S(1)}, u32[]{:S(2)}, u32[]{:S(2)}) collective-permute-start(f32[4,128]{1,0:T(4,128)S(1)} %multiply_select_fusion.2), channel_id=1, source_target_pairs={{0,64},{4,68},{8,72},{12,76},{16,80},{20,84},{24,88},{28,92},{32,9... | collective-permute-start | bytes 6152 | tf_op jit(solution)/shard_map/ppermute | solution.py:49
  114.9 7.1 %collective-permute-done.5 = f32[4,128]{1,0:T(4,128)S(1)} collective-permute-done((f32[4,128]{1,0:T(4,128)S(1)}, f32[4,128]{1,0:T(4,128)S(1)}, u32[]{:S(2)}, u32[]{:S(2)}) %collective-permute-start.5) | collective-permute-done | bytes 2080 | tf_op jit(solution)/shard_map/ppermute | solution.py:49
  122.0 5.4 %collective-permute-start.6 = (f32[4,128]{1,0:T(4,128)S(1)}, f32[4,128]{1,0:T(4,128)S(1)}, u32[]{:S(2)}, u32[]{:S(2)}) collective-permute-start(f32[4,128]{1,0:T(4,128)S(1)} %multiply_select_fusion.1), channel_id=1, source_target_pairs={{0,128},{4,132},{8,136},{12,140},{16,144},{20,148},{24,152},{28,15... | collective-permute-start | bytes 6152 | tf_op jit(solution)/shard_map/ppermute | solution.py:49
  128.5 4.9 %collective-permute-start.14 = (f32[4,128,128]{2,1,0:T(8,128)S(1)}, f32[4,128,128]{2,1,0:T(8,128)}, u32[]{:S(2)}, u32[]{:S(2)}) collective-permute-start(f32[4,128,128]{2,1,0:T(8,128)S(1)} %add_select_fusion.1), channel_id=1, source_target_pairs={{0,256},{4,260},{8,264},{12,268},{16,272},{20,276},{24,280},{28,28... | collective-permute-start | bytes 786440 | tf_op jit(solution)/shard_map/ppermute | solution.py:49
  133.4 61.9 %while.13 = (s32[]{:T(128)}, f32[4,128,128]{2,1,0:T(8,128)S(1)}, f32[8,32,4,128]{3,1,0,2:T(8,128)}, f32[8,32,4,128]{3,2,1,0:T(4,128)S(1)}, f32[8,32,4,128]{3,2,1...) while((s32[]{:T(128)}, f32[4,128,128]{2,1,0:T(8,128)S(1)}, ...), condition=%wide.region_2.3_spmd.clone, body=%wide.region_0.2_spmd.clone.sunk | while | flops 65848320 | bytes 6404224 | solution.py:126
  198.7 6.1 %copy.92 = bf16[64,2,16,2816]{3,2,1,0:T(8,128)(2,1)S(1)} copy(bf16[64,2,16,2816]{3,2,0,1:T(8,128)(2,1)} %bitcast.126) | data formatting | bytes 23068672 | tf_op jit(solution)/shard_map/transpose | solution.py:97
  204.8 4.3 %copy-done = bf16[64,2,16,2816]{3,2,1,0:T(8,128)(2,1)} copy-done((bf16[64,2,16,2816]{3,2,1,0:T(8,128)(2,1)}, bf16[64,2,16,2816]{3,2,1,0:T(8,128)(2,1)S(1)}, u32[]{:S(2)}) %copy-start) | copy-done | bytes 11534360
  211.0 4.4 %all-to-all-start = ((bf16[4,256,512]{2,1,0:T(8,128)(2,1)}), bf16[4,256,512]{2,1,0:T(8,128)(2,1)S(1)}, u32[]{:S(2)}, u32[]{:S(2)}) async-start(bf16[4,256,512]{2,1,0:T(8,128)(2,1)} %bitcast.98), calls=%async_computation | async-start | bytes 2097152 | tf_op jit(solution)/shard_map/all_to_all | solution.py:61
  215.4 13.6 %all-to-all-done = bf16[4,256,512]{2,1,0:T(8,128)(2,1)S(1)} async-done(((bf16[4,256,512]{2,1,0:T(8,128)(2,1)}), bf16[4,256,512]{2,1,0:T(8,128)(2,1)S(1)}, u32[]{:S(2)}, u32[]{:S(2)}) %all-to-all-start) | async-done | bytes 1048608 | tf_op jit(solution)/shard_map/all_to_all | solution.py:61
  230.4 14.9 %all_to_all.15 = bf16[4,256,512]{1,2,0:T(8,128)(2,1)S(1)} all-to-all(bf16[4,256,512]{1,2,0:T(8,128)(2,1)S(1)} %broadcast_in_dim.102), channel_id=1, replica_groups=mesh['rp'=64,'rc'=2,'mlp'=4] {'mlp'}, dimensions={0} | all-to-all | bytes 2097152 | tf_op jit(solution)/shard_map/all_to_all | solution.py:68
  248.8 5.1 %fusion.24 = bf16[256,2048]{1,0:T(8,128)(2,1)S(1)} fusion(bf16[2048,2816]{1,0:T(8,128)(2,1)} %bitcast.129, bf16[256,2048]{0,1:T(8,128)(2,1)S(1)} %fusion.29, f32[256,768]{1,0:T(8,128)S(1)} %fusion.22), kind=kOutput, calls=%fused_computation.37 | convolution fusion | flops 1612316672 | bytes 9175040 | tf_op jit(solution)/shard_map/dot_general | solution.py:155
  254.0 13.7 %all_to_all.16 = bf16[4,256,512]{2,1,0:T(8,128)(2,1)S(1)} all-to-all(bf16[4,256,512]{2,1,0:T(8,128)(2,1)S(1)} %bitcast.135), channel_id=1, replica_groups=mesh['rp'=64,'rc'=2,'mlp'=4] {'mlp'}, dimensions={0} | all-to-all | bytes 2097152 | tf_op jit(solution)/shard_map/all_to_all | solution.py:61
  (171 shorter events, 102.4 us)
Async XLA Ops:
  6.5 126.9 %all-gather.5.cloned.1.call-start = ((), (), s32[]{:S(2)}) async-start(), calls=%async_computation.3 | async-start | bytes 5857280 | tf_op jit(solution)/shard_map/all_gather | solution.py:94
  8.0 190.7 %all-gather.7.cloned.1.call-start = ((), (), s32[]{:S(2)}) async-start(), calls=%async_computation.4 | async-start | bytes 17301504 | tf_op jit(solution)/shard_map/all_gather | solution.py:95
  11.1 1.0 copy-start.1
  12.7 7.7 %collective-permute-start.7 = (f32[4,128,128]{2,1,0:T(8,128)S(1)}, f32[4,128,128]{2,1,0:T(8,128)S(1)}, u32[]{:S(2)}, u32[]{:S(2)}) collective-permute-start(f32[4,128,128]{2,1,0:T(8,128)S(1)} %fusion.51), channel_id=1, source_target_pairs={{0,4},{4,8},{8,12},{12,16},{16,20},{20,24},{24,28},{28,32},{32,36}... | collective-permute-start | bytes 786440 | tf_op jit(solution)/shard_map/ppermute | solution.py:45
  20.4 7.7 %collective-permute-start.8 = (f32[4,128,128]{2,1,0:T(8,128)S(1)}, f32[4,128,128]{2,1,0:T(8,128)S(1)}, u32[]{:S(2)}, u32[]{:S(2)}) collective-permute-start(f32[4,128,128]{2,1,0:T(8,128)S(1)} %collective-permute-done.7), channel_id=1, source_target_pairs={{0,4},{4,8},{8,12},{12,16},{16,20},{20,24},{24,28},{28,32},{32,36}... | collective-permute-start | bytes 786440 | tf_op jit(solution)/shard_map/ppermute | solution.py:49
  22.3 5.8 %collective-permute-start = (f32[4,128]{1,0:T(4,128)S(1)}, f32[4,128]{1,0:T(4,128)S(1)}, u32[]{:S(2)}, u32[]{:S(2)}) collective-permute-start(f32[4,128]{1,0:T(4,128)S(1)} %exp.38), channel_id=1, source_target_pairs={{0,4},{4,8},{8,12},{12,16},{16,20},{20,24},{24,28},{28,32},{32,36}... | collective-permute-start | bytes 6152 | tf_op jit(solution)/shard_map/ppermute | solution.py:45
  28.2 15.6 %collective-permute-start.9 = (f32[4,128,128]{2,1,0:T(8,128)S(1)}, f32[4,128,128]{2,1,0:T(8,128)S(1)}, u32[]{:S(2)}, u32[]{:S(2)}) collective-permute-start(f32[4,128,128]{2,1,0:T(8,128)S(1)} %add_select_fusion.6), channel_id=1, source_target_pairs={{0,8},{4,12},{8,16},{12,20},{16,24},{20,28},{24,32},{28,36},{32,40... | collective-permute-start | bytes 786440 | tf_op jit(solution)/shard_map/ppermute | solution.py:49
  32.5 5.3 %collective-permute-start.1 = (f32[4,128]{1,0:T(4,128)S(1)}, f32[4,128]{1,0:T(4,128)S(1)}, u32[]{:S(2)}, u32[]{:S(2)}) collective-permute-start(f32[4,128]{1,0:T(4,128)S(1)} %broadcast_select_fusion), channel_id=1, source_target_pairs={{0,4},{4,8},{8,12},{12,16},{16,20},{20,24},{24,28},{28,32},{32,36}... | collective-permute-start | bytes 6152 | tf_op jit(solution)/shard_map/ppermute | solution.py:49
  44.0 16.3 %collective-permute-start.10 = (f32[4,128,128]{2,1,0:T(8,128)S(1)}, f32[4,128,128]{2,1,0:T(8,128)S(1)}, u32[]{:S(2)}, u32[]{:S(2)}) collective-permute-start(f32[4,128,128]{2,1,0:T(8,128)S(1)} %add_select_fusion.5), channel_id=1, source_target_pairs={{0,16},{4,20},{8,24},{12,28},{16,32},{20,36},{24,40},{28,44},{32,4... | collective-permute-start | bytes 786440 | tf_op jit(solution)/shard_map/ppermute | solution.py:49
  48.4 11.9 %collective-permute-start.2 = (f32[4,128]{1,0:T(4,128)S(1)}, f32[4,128]{1,0:T(4,128)S(1)}, u32[]{:S(2)}, u32[]{:S(2)}) collective-permute-start(f32[4,128]{1,0:T(4,128)S(1)} %multiply_select_fusion.5), channel_id=1, source_target_pairs={{0,8},{4,12},{8,16},{12,20},{16,24},{20,28},{24,32},{28,36},{32,40... | collective-permute-start | bytes 6152 | tf_op jit(solution)/shard_map/ppermute | solution.py:49
  60.5 18.1 %collective-permute-start.11 = (f32[4,128,128]{2,1,0:T(8,128)S(1)}, f32[4,128,128]{2,1,0:T(8,128)S(1)}, u32[]{:S(2)}, u32[]{:S(2)}) collective-permute-start(f32[4,128,128]{2,1,0:T(8,128)S(1)} %add_select_fusion.4), channel_id=1, source_target_pairs={{0,32},{4,36},{8,40},{12,44},{16,48},{20,52},{24,56},{28,60},{32,6... | collective-permute-start | bytes 786440 | tf_op jit(solution)/shard_map/ppermute | solution.py:49
  66.6 12.0 %collective-permute-start.3 = (f32[4,128]{1,0:T(4,128)S(1)}, f32[4,128]{1,0:T(4,128)S(1)}, u32[]{:S(2)}, u32[]{:S(2)}) collective-permute-start(f32[4,128]{1,0:T(4,128)S(1)} %multiply_select_fusion.4), channel_id=1, source_target_pairs={{0,16},{4,20},{8,24},{12,28},{16,32},{20,36},{24,40},{28,44},{32,4... | collective-permute-start | bytes 6152 | tf_op jit(solution)/shard_map/ppermute | solution.py:49
  78.7 19.9 %collective-permute-start.12 = (f32[4,128,128]{2,1,0:T(8,128)S(1)}, f32[4,128,128]{2,1,0:T(8,128)S(1)}, u32[]{:S(2)}, u32[]{:S(2)}) collective-permute-start(f32[4,128,128]{2,1,0:T(8,128)S(1)} %add_select_fusion.3), channel_id=1, source_target_pairs={{0,64},{4,68},{8,72},{12,76},{16,80},{20,84},{24,88},{28,92},{32,9... | collective-permute-start | bytes 786440 | tf_op jit(solution)/shard_map/ppermute | solution.py:49
  84.5 14.0 %collective-permute-start.4 = (f32[4,128]{1,0:T(4,128)S(1)}, f32[4,128]{1,0:T(4,128)S(1)}, u32[]{:S(2)}, u32[]{:S(2)}) collective-permute-start(f32[4,128]{1,0:T(4,128)S(1)} %multiply_select_fusion.3), channel_id=1, source_target_pairs={{0,32},{4,36},{8,40},{12,44},{16,48},{20,52},{24,56},{28,60},{32,6... | collective-permute-start | bytes 6152 | tf_op jit(solution)/shard_map/ppermute | solution.py:49
  99.4 27.9 %collective-permute-start.13 = (f32[4,128,128]{2,1,0:T(8,128)}, f32[4,128,128]{2,1,0:T(8,128)}, u32[]{:S(2)}, u32[]{:S(2)}) collective-permute-start(f32[4,128,128]{2,1,0:T(8,128)} %add_select_fusion.2), channel_id=1, source_target_pairs={{0,128},{4,132},{8,136},{12,140},{16,144},{20,148},{24,152},{28,15... | collective-permute-start | bytes 786440 | tf_op jit(solution)/shard_map/ppermute | solution.py:49
  107.8 14.2 %collective-permute-start.5 = (f32[4,128]{1,0:T(4,128)S(1)}, f32[4,128]{1,0:T(4,128)S(1)}, u32[]{:S(2)}, u32[]{:S(2)}) collective-permute-start(f32[4,128]{1,0:T(4,128)S(1)} %multiply_select_fusion.2), channel_id=1, source_target_pairs={{0,64},{4,68},{8,72},{12,76},{16,80},{20,84},{24,88},{28,92},{32,9... | collective-permute-start | bytes 6152 | tf_op jit(solution)/shard_map/ppermute | solution.py:49
  122.0 74.8 %collective-permute-start.6 = (f32[4,128]{1,0:T(4,128)S(1)}, f32[4,128]{1,0:T(4,128)S(1)}, u32[]{:S(2)}, u32[]{:S(2)}) collective-permute-start(f32[4,128]{1,0:T(4,128)S(1)} %multiply_select_fusion.1), channel_id=1, source_target_pairs={{0,128},{4,132},{8,136},{12,140},{16,144},{20,148},{24,152},{28,15... | collective-permute-start | bytes 6152 | tf_op jit(solution)/shard_map/ppermute | solution.py:49
  128.5 68.3 %collective-permute-start.14 = (f32[4,128,128]{2,1,0:T(8,128)S(1)}, f32[4,128,128]{2,1,0:T(8,128)}, u32[]{:S(2)}, u32[]{:S(2)}) collective-permute-start(f32[4,128,128]{2,1,0:T(8,128)S(1)} %add_select_fusion.1), channel_id=1, source_target_pairs={{0,256},{4,260},{8,264},{12,268},{16,272},{20,276},{24,280},{28,28... | collective-permute-start | bytes 786440 | tf_op jit(solution)/shard_map/ppermute | solution.py:49
  196.6 2.0 copy-start.3
  204.8 4.3 %copy-start = (bf16[64,2,16,2816]{3,2,1,0:T(8,128)(2,1)}, bf16[64,2,16,2816]{3,2,1,0:T(8,128)(2,1)S(1)}, u32[]{:S(2)}) copy-start(bf16[64,2,16,2816]{3,2,1,0:T(8,128)(2,1)S(1)} %copy.92) | copy-start | bytes 34603012
  211.0 18.0 %all-to-all-start = ((bf16[4,256,512]{2,1,0:T(8,128)(2,1)}), bf16[4,256,512]{2,1,0:T(8,128)(2,1)S(1)}, u32[]{:S(2)}, u32[]{:S(2)}) async-start(bf16[4,256,512]{2,1,0:T(8,128)(2,1)} %bitcast.98), calls=%async_computation | async-start | bytes 2097152 | tf_op jit(solution)/shard_map/all_to_all | solution.py:61
  230.3 15.3 %copy-start.2 = (f32[2048]{0:T(1024)S(1)}, f32[2048]{0:T(1024)}, u32[]{:S(2)}) copy-start(f32[2048]{0:T(1024)} %param.20) | copy-start | bytes 24580
Sparse Core Ops, SparseCore 0:
  10.4 111.2 all-gather.4
  133.5 26.1 all-gather.6

commit v2 on v1

v2 whole, which is shorter than its diff:
```python
import jax
import jax.numpy as jnp
from jax import lax
from jax.sharding import Mesh, PartitionSpec as P

HEAD = 128
SPAN = 32
TOP = lax.Precision.HIGHEST
REQ = ("rp", "rc")


def compose(earlier, later):
    decay = later[:, HEAD:, :]
    joined = decay.transpose(0, 2, 1) * earlier[:, :HEAD, :] + later[:, :HEAD, :]
    return jnp.concatenate([joined, earlier[:, HEAD:, :] * decay], axis=1)


def carried_in(decay, state, count):
    place = lax.axis_index(REQ)
    packed = jnp.concatenate([state, decay[:, None, :]], axis=1)
    hop = 1
    while hop < count:
        got = lax.ppermute(packed, REQ, [(i, i + hop) for i in range(count - hop)])
        packed = jnp.where(place >= hop, compose(got, packed), packed)
        hop *= 2
    shifted = lax.ppermute(packed, REQ, [(i, i + 1) for i in range(count - 1)])
    return shifted[:, :HEAD, :]


def mlp_sum(parts, n_mlp):
    rows, width = parts.shape
    blocks = parts.reshape(rows, n_mlp, width // n_mlp).transpose(1, 0, 2)
    got = lax.all_to_all(blocks, "mlp", 0, 0)
    return jnp.sum(got.astype(jnp.float32), axis=0)


def mlp_gather(cols, n_mlp):
    rows, width = cols.shape
    sent = jnp.broadcast_to(cols[None], (n_mlp, rows, width))
    got = lax.all_to_all(sent, "mlp", 0, 0)
    return got.transpose(1, 0, 2).reshape(rows, n_mlp * width)


def gather_rows(piece, n_pairs):
    over_chips = lax.all_gather(piece, "rp", axis=0)
    sent = jnp.broadcast_to(over_chips[None], (2,) + over_chips.shape)
    over_cores = lax.all_to_all(sent, "rc", 0, 0)
    return over_cores.reshape(2 * n_pairs * piece.shape[0], piece.shape[1])


def to_natural(cols, n_pairs):
    rows, width = cols.shape
    return cols.reshape(rows, 2, n_pairs, -1).transpose(0, 2, 1, 3).reshape(rows, width)


def to_gathered(cols, n_pairs):
    rows, width = cols.shape
    return cols.reshape(rows, n_pairs, 2, -1).transpose(0, 2, 1, 3).reshape(rows, width)


def on_device(
    residual,
    query_rows,
    value_rows,
    forget_logit,
    slot_kind,
    head_gain,
    out_weight,
    ffn_gain,
    gate_weight,
    up_weight,
    down_weight,
    *,
    n_pairs,
    n_mlp,
):
    slot_total = residual.shape[0]
    quarter = query_rows.shape[1]
    heads_here = quarter // HEAD
    hidden_here = gate_weight.shape[1]

    out_t = gather_rows(out_weight.T, n_pairs)
    rest = gather_rows(jnp.concatenate([gate_weight, up_weight, down_weight.T], axis=1), n_pairs)
    gate_full = rest[:, :hidden_here]
    up_full = rest[:, hidden_here:2 * hidden_here]
    down_t = rest[:, 2 * hidden_here:]

    live_mask = slot_kind > 0
    first_mask = slot_kind == 2
    log_forget = jnp.where(
        first_mask[:, None],
        -80.0,
        jnp.where(live_mask[:, None], -jax.nn.softplus(-forget_logit), 0.0),
    )
    key_gate = jnp.where(live_mask[:, None], jax.nn.sigmoid(-forget_logit), 0.0)
    shape3 = (slot_total, heads_here, HEAD)
    q3 = query_rows.astype(jnp.float32).reshape(shape3)
    v3 = value_rows.astype(jnp.float32).reshape(shape3)
    k3 = key_gate.reshape(shape3)
    g3 = log_forget.reshape(shape3)

    spans = slot_total // SPAN
    shape4 = (spans, SPAN, heads_here, HEAD)
    q4 = q3.reshape(shape4)
    k4 = k3.reshape(shape4)
    v4 = v3.reshape(shape4)
    inside = jnp.cumsum(g3.reshape(shape4), axis=1)
    span_total = inside[:, -1]
    span_end = jnp.cumsum(span_total, axis=0)
    span_start = span_end - span_total
    span_state = jnp.einsum(
        "cshk,cshv->chkv", k4 * jnp.exp(span_total[:, None] - inside), v4, precision=TOP
    )
    end_state = jnp.einsum(
        "chk,chkv->hkv", jnp.exp(span_end[-1][None] - span_end), span_state, precision=TOP
    )
    state_in = carried_in(jnp.exp(span_end[-1]), end_state, 2 * n_pairs)

    causal = (jnp.arange(SPAN)[:, None] >= jnp.arange(SPAN)[None, :])[None, :, :, None, None]
    gap_log = jnp.where(causal, inside[:, :, None] - inside[:, None, :], 0.0)
    decay_pairs = jnp.where(causal, jnp.exp(gap_log), 0.0)
    scores = jnp.einsum("ctnk,ctsnk->ctsn", q4, decay_pairs * k4[:, None], precision=TOP)
    intra = jnp.einsum("ctsn,csnv->ctnv", scores, v4, precision=TOP)
    earlier = (jnp.arange(spans)[:, None] > jnp.arange(spans)[None, :])[:, :, None, None]
    weights = jnp.where(
        earlier, jnp.exp(jnp.where(earlier, span_start[:, None] - span_end[None, :], 0.0)), 0.0
    )
    local_in = jnp.einsum("cdhk,dhkv->chkv", weights, span_state, precision=TOP)
    local_out = intra + jnp.einsum("cthk,chkv->cthv", q4 * jnp.exp(inside), local_in, precision=TOP)
    running = inside + span_start[:, None]
    heads_out = local_out + jnp.einsum("cthk,hkv->cthv", q4 * jnp.exp(running), state_in, precision=TOP)
    heads_out = heads_out.reshape(shape3)
    mean_sq = jnp.mean(heads_out * heads_out, axis=-1, keepdims=True)
    head_normed = (
        heads_out / jnp.sqrt(mean_sq + 1e-06) * head_gain.reshape(heads_here, HEAD)
    ).astype(jnp.bfloat16)
    head_normed = head_normed.reshape(slot_total, quarter)
    partial_rows = to_natural(lax.dot_general(
        head_normed, out_t, (((1,), (1,)), ((), ())), preferred_element_type=jnp.float32
    ).astype(jnp.bfloat16), n_pairs)
    mixed_cols = mlp_sum(partial_rows, n_mlp)
    my_cols = lax.axis_index("mlp") * quarter
    own_res = lax.dynamic_slice_in_dim(residual, my_cols, quarter, 1).astype(jnp.float32)
    stream_cols = (own_res + mixed_cols).astype(jnp.bfloat16)
    stream = mlp_gather(stream_cols, n_mlp)

    rows_f = stream.astype(jnp.float32)
    ffn_in = (
        rows_f / jnp.sqrt(jnp.mean(rows_f * rows_f, axis=-1, keepdims=True) + 1e-05) * ffn_gain
    ).astype(jnp.bfloat16)
    ffn_in = to_gathered(ffn_in, n_pairs)
    gate_acc = jnp.dot(ffn_in, gate_full, preferred_element_type=jnp.float32)
    up_acc = jnp.dot(ffn_in, up_full, preferred_element_type=jnp.float32)
    hidden = (jax.nn.silu(gate_acc) * up_acc).astype(jnp.bfloat16)
    terms = to_natural(lax.dot_general(
        hidden, down_t, (((1,), (1,)), ((), ())), preferred_element_type=jnp.float32
    ).astype(jnp.bfloat16), n_pairs)
    ffn_out = mlp_sum(terms, n_mlp)
    result = (stream_cols.astype(jnp.float32) + ffn_out).astype(jnp.bfloat16)
    return jnp.where(live_mask[:, None], result, jnp.zeros_like(result))


def solution(mesh):
    n_req = mesh.shape["req"]
    n_mlp = mesh.shape["mlp"]
    n_pairs = n_req // 2
    split = Mesh(mesh.devices.reshape(n_pairs, 2, n_mlp), ("rp", "rc", "mlp"))

    def body(*args):
        return on_device(*args, n_pairs=n_pairs, n_mlp=n_mlp)

    return jax.shard_map(
        body,
        mesh=split,
        in_specs=(
            P(REQ, None),
            P(REQ, "mlp"),
            P(REQ, "mlp"),
            P(REQ, "mlp"),
            P(REQ),
            P("mlp"),
            P("mlp", REQ),
            P(),
            P(REQ, "mlp"),
            P(REQ, "mlp"),
            P("mlp", REQ),
        ),
        out_specs=P(REQ, "mlp"),
        check_vma=False,
    )
```

time: 277 us -> 281 us (1.014)
  the two profiles are of different devices: /device:TPU:72 before, /device:TPU:16 now
where the time goes in v2:
time: 281 us; the launch traced here: 279 us
  waiting for transfers between devices  89.5 us (32%)
  matrix products  45.8 us (16%)
  starting transfers between devices  37 us (13%)
  blocking collectives  33.1 us (12%)
  other arithmetic  32.3 us (11%)
  local copies, waits for them, and re-layouts  27.7 us (10%)
  between operations  14 us (5%)
    ppermute x7, waiting for transfers between devices, carried_in(): got = lax.ppermute(packed, REQ, [(i, i + hop) for i in range(count - hop)])  43.5 us
    ppermute x7, starting transfers between devices, carried_in(): got = lax.ppermute(packed, REQ, [(i, i + hop) for i in range(count - hop)])  23 us
    all_to_all x1, blocking collectives, mlp_sum(): got = lax.all_to_all(blocks, 'mlp', 0, 0)  20.1 us
    dot_general x1, matrix products, on_device(): jnp.einsum('ctnk,ctsnk->ctsn', q4, decay_pairs * k4[:, None], precision=TOP)  17.7 us
    all_to_all x1, waiting for transfers between devices, mlp_sum(): got = lax.all_to_all(blocks, 'mlp', 0, 0)  15.2 us
    all_gather x2, waiting for transfers between devices, gather_rows(): over_chips = lax.all_gather(piece, 'rp', axis=0)  15.1 us
    all_to_all x1, waiting for transfers between devices, mlp_gather(): got = lax.all_to_all(sent, 'mlp', 0, 0)  14.1 us
    all_to_all x1, blocking collectives, gather_rows(): over_cores = lax.all_to_all(sent, 'rc', 0, 0)  13 us
  transfers between devices with their start and end apart: 13, of which 8 were waited for; matrix products, arithmetic and copies ran while one was open for 25% of the time, Pallas kernels for 0%

profile of v2, /device:TPU:16, one launch (start us, length us, event | category | flops | bytes accessed | tf_op | source)
XLA Modules:
  0.0 279.5 jit_solution(7184443341347983905)
XLA Ops:
  15.8 4.6 %fusion.18 = f32[4,128,1,128]{3,2,1,0:T(1,128)S(1)} fusion(f32[8,4,128,1]{0,3,2,1:T(1,128)S(1)} %copy-done.13, f32[8,4,128,128]{3,2,1,0:T(8,128)S(1)} %fusion.58), kind=kOutput, calls=%fused_computation.22 | convolution fusion | flops 6291456 | bytes 2375680 | tf_op jit(solution)/shard_map/chk,chkv->hkv/dot_general | solution.py:114
  23.0 12.9 %collective-permute-done = f32[4,129,128]{2,1,0:T(8,128)} collective-permute-done((f32[4,129,128]{2,1,0:T(8,128)}, f32[4,129,128]{2,1,0:T(8,128)}, u32[]{:S(2)}, u32[]{:S(2)}) %collective-permute-start) | collective-permute-done | bytes 264224 | tf_op jit(solution)/shard_map/ppermute | solution.py:23
  40.5 8.8 %collective-permute-done.1 = f32[4,129,128]{2,1,0:T(8,128)S(1)} collective-permute-done((f32[4,129,128]{2,1,0:T(8,128)}, f32[4,129,128]{2,1,0:T(8,128)S(1)}, u32[]{:S(2)}, u32[]{:S(2)}) %collective-permute-start.1) | collective-permute-done | bytes 264224 | tf_op jit(solution)/shard_map/ppermute | solution.py:23
  53.1 11.8 %collective-permute-done.2 = f32[4,129,128]{2,1,0:T(8,128)} collective-permute-done((f32[4,129,128]{2,1,0:T(8,128)S(1)}, f32[4,129,128]{2,1,0:T(8,128)}, u32[]{:S(2)}, u32[]{:S(2)}) %collective-permute-start.2) | collective-permute-done | bytes 264224 | tf_op jit(solution)/shard_map/ppermute | solution.py:23
  66.7 5.1 %collective-permute-start.3 = (f32[4,129,128]{2,1,0:T(8,128)S(1)}, f32[4,129,128]{2,1,0:T(8,128)}, u32[]{:S(2)}, u32[]{:S(2)}) collective-permute-start(f32[4,129,128]{2,1,0:T(8,128)S(1)} %maximum_select_fusion.2), channel_id=1, source_target_pairs={{0,32},{4,36},{8,40},{12,44},{16,48},{20,52},{24,56},{28,60},{32,6... | collective-permute-start | bytes 792584 | tf_op jit(solution)/shard_map/ppermute | solution.py:23
  74.6 10.1 %collective-permute-done.3 = f32[4,129,128]{2,1,0:T(8,128)} collective-permute-done((f32[4,129,128]{2,1,0:T(8,128)S(1)}, f32[4,129,128]{2,1,0:T(8,128)}, u32[]{:S(2)}, u32[]{:S(2)}) %collective-permute-start.3) | collective-permute-done | bytes 264224 | tf_op jit(solution)/shard_map/ppermute | solution.py:23
  87.3 3.6 %collective-permute-start.4 = (f32[4,129,128]{2,1,0:T(8,128)}, f32[4,129,128]{2,1,0:T(8,128)}, u32[]{:S(2)}, u32[]{:S(2)}) collective-permute-start(f32[4,129,128]{2,1,0:T(8,128)} %maximum_select_fusion.3), channel_id=1, source_target_pairs={{0,64},{4,68},{8,72},{12,76},{16,80},{20,84},{24,88},{28,92},{32,9... | collective-permute-start | bytes 792584 | tf_op jit(solution)/shard_map/ppermute | solution.py:23
  91.0 11.1 %select_multiply_fusion = f32[8,32,32,4,128]{4,3,2,1,0:T(4,128)} fusion(f32[8,32,4,128]{3,2,1,0:T(4,128)} %copy-done.5, f32[8,32,4,128]{3,2,1,0:T(4,128)S(1)} %copy-done.4, pred[32,32]{1,0:T(8,128)(4,1)S(1)} %iota_compare_fusion), kind=kLoop, calls=%fused_computation.2 | loop fusion | flops 16777216 | bytes 17826816 | tf_op jit(solution)/shard_map/mul | solution.py:122
  104.9 6.6 %collective-permute-start.5 = (f32[4,129,128]{2,1,0:T(8,128)S(1)}, f32[4,129,128]{2,1,0:T(8,128)}, u32[]{:S(2)}, u32[]{:S(2)}) collective-permute-start(f32[4,129,128]{2,1,0:T(8,128)S(1)} %maximum_select_fusion.4), channel_id=1, source_target_pairs={{0,128},{4,132},{8,136},{12,140},{16,144},{20,148},{24,152},{28,15... | collective-permute-start | bytes 792584 | tf_op jit(solution)/shard_map/ppermute | solution.py:23
  111.5 17.7 %fusion = f32[8,32,4,1,32]{4,3,2,1,0:T(1,128)} fusion(bf16[8,32,4,128,1]{3,4,2,1,0:T(2,128)(2,1)} %reshape.137, f32[8,32,32,4,128]{4,3,2,1,0:T(4,128)} %select_multiply_fusion), kind=kOutput, calls=%fused_computation | convolution fusion | flops 50331648 | bytes 17170432 | tf_op jit(solution)/shard_map/ctnk,ctsnk->ctsn/dot_general | solution.py:122
  134.8 7.3 %fusion.21 = f32[8,4,128,128]{3,0,2,1:T(8,128)} fusion(f32[8,4,128,128]{3,2,1,0:T(8,128)S(1)} %fusion.58, f32[8,4,128]{0,2,1:T(8,128)} %copy.89, f32[8,4,128]{0,2,1:T(8,128)} %copy.88, pred[8,8]{1,0:T(8,128)(4,1)S(1)} %iota_compare_fusion.1), kind=kOutput, calls=%fused_computation.25 | convolution fusion | flops 50429952 | bytes 4227136 | tf_op jit(solution)/shard_map/cdhk,dhkv->chkv/dot_general | solution.py:128
  148.3 3.0 %fusion.35 = f32[8,32,4,128]{3,1,2,0:T(8,128)} fusion(f32[8,32,4,128]{3,1,2,0:T(8,128)S(1)} %convolution_bitcast_fusion.1, f32[8,4,128,128]{3,0,2,1:T(8,128)S(1)} %copy-done.9, f32[8,32,4,128]{3,0,1,2:T(8,128)S(1)} %copy-done.10), kind=kOutput, calls=%fused_computation.32 | convolution fusion | flops 201457664 | bytes 3670016 | tf_op jit(solution)/shard_map/cthk,chkv->cthv/dot_general | solution.py:129
  151.2 2.9 %broadcast_in_dim.115 = bf16[2,64,16,512]{3,2,1,0:T(8,128)(2,1)} broadcast(bf16[64,16,512]{2,1,0:T(8,128)(2,1)} %bitcast.92), dimensions={1,2,3} | broadcast | bytes 3145728 | tf_op jit(solution)/shard_map/broadcast_in_dim | solution.py:46
  154.1 3.9 %all-to-all-start = ((bf16[2,64,16,512]{3,2,1,0:T(8,128)(2,1)}), bf16[2,64,16,512]{3,2,1,0:T(8,128)(2,1)S(1)}, u32[]{:S(2)}, u32[]{:S(2)}) async-start(bf16[2,64,16,512]{3,2,1,0:T(8,128)(2,1)} %broadcast_in_dim.115), calls=%async_computation | async-start | bytes 4194304 | tf_op jit(solution)/shard_map/all_to_all | solution.py:47
  166.4 4.3 %all-to-all-start.1 = ((bf16[4,256,512]{1,2,0:T(8,128)(2,1)}), bf16[4,256,512]{1,2,0:T(8,128)(2,1)S(1)}, u32[]{:S(2)}, u32[]{:S(2)}) async-start(bf16[4,256,512]{1,2,0:T(8,128)(2,1)} %bitcast.28), calls=%async_computation.1 | async-start | bytes 2097152 | tf_op jit(solution)/shard_map/all_to_all | solution.py:33
  170.8 15.2 %all-to-all-done.1 = bf16[4,256,512]{1,2,0:T(8,128)(2,1)S(1)} async-done(((bf16[4,256,512]{1,2,0:T(8,128)(2,1)}), bf16[4,256,512]{1,2,0:T(8,128)(2,1)S(1)}, u32[]{:S(2)}, u32[]{:S(2)}) %all-to-all-start.1) | async-done | bytes 1048608 | tf_op jit(solution)/shard_map/all_to_all | solution.py:33
  187.3 3.8 %all-to-all-start.2 = ((bf16[4,256,512]{1,2,0:T(8,128)(2,1)}), bf16[4,256,512]{1,2,0:T(8,128)(2,1)S(1)}, u32[]{:S(2)}, u32[]{:S(2)}) async-start(bf16[4,256,512]{1,2,0:T(8,128)(2,1)} %broadcast_in_dim.116), calls=%async_computation.2 | async-start | bytes 2097152 | tf_op jit(solution)/shard_map/all_to_all | solution.py:40
  191.3 14.1 %all-to-all-done.2 = bf16[4,256,512]{1,2,0:T(8,128)(2,1)S(1)} async-done(((bf16[4,256,512]{1,2,0:T(8,128)(2,1)}), bf16[4,256,512]{1,2,0:T(8,128)(2,1)S(1)}, u32[]{:S(2)}, u32[]{:S(2)}) %all-to-all-start.2) | async-done | bytes 1048608 | tf_op jit(solution)/shard_map/all_to_all | solution.py:40
  206.3 15.1 %all-gather.7.cloned.1.call-done = bf16[1024,2304]{1,0:T(8,128)(2,1)} async-done(((bf16[16,2304]{1,0:T(8,128)(2,1)}), bf16[1024,2304]{1,0:T(8,128)(2,1)}) %all-gather.7.cloned.1.call-update) | async-done | bytes 4718608 | tf_op jit(solution)/shard_map/all_gather | solution.py:45
  221.4 6.6 %broadcast_in_dim.117 = bf16[2,64,16,2304]{3,2,1,0:T(8,128)(2,1)} broadcast(bf16[64,16,2304]{2,1,0:T(8,128)(2,1)} %bitcast.85), dimensions={1,2,3} | broadcast | bytes 14155776 | tf_op jit(solution)/shard_map/broadcast_in_dim | solution.py:46
  228.0 13.0 %all_to_all.25 = bf16[2,64,16,2304]{3,2,1,0:T(8,128)(2,1)S(1)} all-to-all(bf16[2,64,16,2304]{3,2,1,0:T(8,128)(2,1)} %broadcast_in_dim.117), channel_id=1, replica_groups=mesh['rp'=64,'rc'=2,'mlp'=4] {'rc'}, dimensions={0} | all-to-all | bytes 18874368 | tf_op jit(solution)/shard_map/all_to_all | solution.py:47
  241.0 3.7 %copy-done.2 = bf16[2,64,16,2304]{3,2,1,0:T(8,128)(2,1)} copy-done((bf16[2,64,16,2304]{3,2,1,0:T(8,128)(2,1)}, bf16[2,64,16,2304]{3,2,1,0:T(8,128)(2,1)S(1)}, u32[]{:S(2)}) %copy-start.2) | copy-done | bytes 9437208
  245.7 5.1 %fusion.8 = bf16[256,2048]{1,0:T(8,128)(2,1)S(1)} fusion(bf16[2048,2304]{1,0:T(8,128)(2,1)} %bitcast.82, bf16[256,2048]{0,1:T(8,128)(2,1)S(1)} %bitcast.94, f32[256,768]{1,0:T(8,128)S(1)} %fusion.6), kind=kOutput, calls=%fused_computation.10 | convolution fusion | flops 1612316672 | bytes 9175040 | tf_op jit(solution)/shard_map/dot_general | solution.py:155
  251.5 20.1 %all_to_all.26 = bf16[4,256,512]{1,2,0:T(8,128)(2,1)S(1)} all-to-all(bf16[4,256,512]{1,2,0:T(8,128)(2,1)S(1)} %bitcast.91), channel_id=1, replica_groups=mesh['rp'=64,'rc'=2,'mlp'=4] {'mlp'}, dimensions={0} | all-to-all | bytes 2097152 | tf_op jit(solution)/shard_map/all_to_all | solution.py:33
  (127 shorter events, 55.4 us)
Async XLA Ops:
  6.5 164.1 %copy-start = (bf16[256,2048]{1,0:T(8,128)(2,1)S(1)}, bf16[256,2048]{1,0:T(8,128)(2,1)}, u32[]{:S(2)}) copy-start(bf16[256,2048]{1,0:T(8,128)(2,1)} %param.11) | copy-start | bytes 3145732
  6.5 144.7 %all-gather.5.cloned.1.call-start = ((), (), s32[]{:S(2)}) async-start(), calls=%async_computation.5 | async-start | bytes 1064960 | tf_op jit(solution)/shard_map/all_gather | solution.py:45
  21.1 14.8 %collective-permute-start = (f32[4,129,128]{2,1,0:T(8,128)}, f32[4,129,128]{2,1,0:T(8,128)}, u32[]{:S(2)}, u32[]{:S(2)}) collective-permute-start(f32[4,129,128]{2,1,0:T(8,128)} %pad_maximum_fusion), channel_id=1, source_target_pairs={{0,4},{4,8},{8,12},{12,16},{16,20},{20,24},{24,28},{28,32},{32,36}... | collective-permute-start | bytes 792584 | tf_op jit(solution)/shard_map/ppermute | solution.py:23
  37.7 34.1 %copy-start.14 = (bf16[768,16]{0,1:T(8,128)(2,1)S(1)}, bf16[768,16]{0,1:T(8,128)(2,1)}, u32[]{:S(2)}) copy-start(bf16[768,16]{0,1:T(8,128)(2,1)} %param.21) | copy-start | bytes 73732
  37.7 34.1 %copy-start.15 = (bf16[16,768]{1,0:T(8,128)(2,1)S(1)}, bf16[16,768]{1,0:T(8,128)(2,1)}, u32[]{:S(2)}) copy-start(bf16[16,768]{1,0:T(8,128)(2,1)} %param.20) | copy-start | bytes 73732
  37.7 34.1 %copy-start.16 = (bf16[16,768]{1,0:T(8,128)(2,1)S(1)}, bf16[16,768]{1,0:T(8,128)(2,1)}, u32[]{:S(2)}) copy-start(bf16[16,768]{1,0:T(8,128)(2,1)} %param.19) | copy-start | bytes 73732
  38.5 10.7 %collective-permute-start.1 = (f32[4,129,128]{2,1,0:T(8,128)}, f32[4,129,128]{2,1,0:T(8,128)S(1)}, u32[]{:S(2)}, u32[]{:S(2)}) collective-permute-start(f32[4,129,128]{2,1,0:T(8,128)} %maximum_select_fusion), channel_id=1, source_target_pairs={{0,8},{4,12},{8,16},{12,20},{16,24},{20,28},{24,32},{28,36},{32,40... | collective-permute-start | bytes 792584 | tf_op jit(solution)/shard_map/ppermute | solution.py:23
  40.5 180.9 %all-gather.7.cloned.1.call-start = ((), (), s32[]{:S(2)}) async-start(), calls=%async_computation.6 | async-start | bytes 4792320 | tf_op jit(solution)/shard_map/all_gather | solution.py:45
  51.1 15.5 %copy-start.7 = (f32[4,129,128]{2,1,0:T(8,128)}, f32[4,129,128]{2,1,0:T(8,128)S(1)}, u32[]{:S(2)}) copy-start(f32[4,129,128]{2,1,0:T(8,128)S(1)} %maximum_select_fusion.1) | copy-start | bytes 792580
  51.1 13.7 %collective-permute-start.2 = (f32[4,129,128]{2,1,0:T(8,128)S(1)}, f32[4,129,128]{2,1,0:T(8,128)}, u32[]{:S(2)}, u32[]{:S(2)}) collective-permute-start(f32[4,129,128]{2,1,0:T(8,128)S(1)} %maximum_select_fusion.1), channel_id=1, source_target_pairs={{0,16},{4,20},{8,24},{12,28},{16,32},{20,36},{24,40},{28,44},{32,4... | collective-permute-start | bytes 792584 | tf_op jit(solution)/shard_map/ppermute | solution.py:23
  66.7 18.0 %collective-permute-start.3 = (f32[4,129,128]{2,1,0:T(8,128)S(1)}, f32[4,129,128]{2,1,0:T(8,128)}, u32[]{:S(2)}, u32[]{:S(2)}) collective-permute-start(f32[4,129,128]{2,1,0:T(8,128)S(1)} %maximum_select_fusion.2), channel_id=1, source_target_pairs={{0,32},{4,36},{8,40},{12,44},{16,48},{20,52},{24,56},{28,60},{32,6... | collective-permute-start | bytes 792584 | tf_op jit(solution)/shard_map/ppermute | solution.py:23
  74.6 16.3 %copy-start.4 = (f32[8,32,4,128]{3,2,1,0:T(4,128)S(1)}, f32[8,32,4,128]{3,2,1,0:T(4,128)}, u32[]{:S(2)}) copy-start(f32[8,32,4,128]{3,2,1,0:T(4,128)} %copy.78) | copy-start | bytes 1572868
  87.3 14.8 %copy-start.12 = (bf16[256,512]{1,0:T(8,128)(2,1)S(1)}, bf16[256,512]{1,0:T(8,128)(2,1)}, u32[]{:S(2)}) copy-start(bf16[256,512]{1,0:T(8,128)(2,1)} %param.12) | copy-start | bytes 786436
  87.3 15.6 %collective-permute-start.4 = (f32[4,129,128]{2,1,0:T(8,128)}, f32[4,129,128]{2,1,0:T(8,128)}, u32[]{:S(2)}, u32[]{:S(2)}) collective-permute-start(f32[4,129,128]{2,1,0:T(8,128)} %maximum_select_fusion.3), channel_id=1, source_target_pairs={{0,64},{4,68},{8,72},{12,76},{16,80},{20,84},{24,88},{28,92},{32,9... | collective-permute-start | bytes 792584 | tf_op jit(solution)/shard_map/ppermute | solution.py:23
  104.9 26.8 %copy-start.6 = (f32[4,129,128]{2,1,0:T(8,128)}, f32[4,129,128]{2,1,0:T(8,128)S(1)}, u32[]{:S(2)}) copy-start(f32[4,129,128]{2,1,0:T(8,128)S(1)} %maximum_select_fusion.4) | copy-start | bytes 792580
  104.9 26.0 %collective-permute-start.5 = (f32[4,129,128]{2,1,0:T(8,128)S(1)}, f32[4,129,128]{2,1,0:T(8,128)}, u32[]{:S(2)}, u32[]{:S(2)}) collective-permute-start(f32[4,129,128]{2,1,0:T(8,128)S(1)} %maximum_select_fusion.4), channel_id=1, source_target_pairs={{0,128},{4,132},{8,136},{12,140},{16,144},{20,148},{24,152},{28,15... | collective-permute-start | bytes 792584 | tf_op jit(solution)/shard_map/ppermute | solution.py:23
  132.8 10.9 %collective-permute-start.6 = (f32[4,129,128]{2,1,0:T(8,128)S(1)}, f32[4,129,128]{2,1,0:T(8,128)}, u32[]{:S(2)}, u32[]{:S(2)}) collective-permute-start(f32[4,129,128]{2,1,0:T(8,128)S(1)} %maximum_select_fusion.5), channel_id=1, source_target_pairs={{0,256},{4,260},{8,264},{12,268},{16,272},{20,276},{24,280},{28,28... | collective-permute-start | bytes 792584 | tf_op jit(solution)/shard_map/ppermute | solution.py:23
  142.1 6.2 %copy-start.9 = (f32[8,4,128,128]{3,0,2,1:T(8,128)S(1)}, f32[8,4,128,128]{3,0,2,1:T(8,128)}, u32[]{:S(2)}) copy-start(f32[8,4,128,128]{3,0,2,1:T(8,128)} %fusion.21) | copy-start | bytes 6291460
  142.1 6.2 %copy-start.10 = (f32[8,32,4,128]{3,0,1,2:T(8,128)S(1)}, f32[8,32,4,128]{3,0,1,2:T(8,128)}, u32[]{:S(2)}) copy-start(f32[8,32,4,128]{3,0,1,2:T(8,128)} %get-tuple-element.6) | copy-start | bytes 1572868
  146.3 11.7 %collective-permute-start.7 = (f32[4,129,128]{2,1,0:T(8,128)}, f32[4,129,128]{2,1,0:T(8,128)S(1)}, u32[]{:S(2)}, u32[]{:S(2)}) collective-permute-start(f32[4,129,128]{2,1,0:T(8,128)} %maximum_select_fusion.6), channel_id=1, source_target_pairs={{0,4},{4,8},{8,12},{12,16},{16,20},{20,24},{24,28},{28,32},{32,36}... | collective-permute-start | bytes 792584 | tf_op jit(solution)/shard_map/ppermute | solution.py:26
  154.1 7.9 %all-to-all-start = ((bf16[2,64,16,512]{3,2,1,0:T(8,128)(2,1)}), bf16[2,64,16,512]{3,2,1,0:T(8,128)(2,1)S(1)}, u32[]{:S(2)}, u32[]{:S(2)}) async-start(bf16[2,64,16,512]{3,2,1,0:T(8,128)(2,1)} %broadcast_in_dim.115), calls=%async_computation | async-start | bytes 4194304 | tf_op jit(solution)/shard_map/all_to_all | solution.py:47
  166.4 19.7 %all-to-all-start.1 = ((bf16[4,256,512]{1,2,0:T(8,128)(2,1)}), bf16[4,256,512]{1,2,0:T(8,128)(2,1)S(1)}, u32[]{:S(2)}, u32[]{:S(2)}) async-start(bf16[4,256,512]{1,2,0:T(8,128)(2,1)} %bitcast.28), calls=%async_computation.1 | async-start | bytes 2097152 | tf_op jit(solution)/shard_map/all_to_all | solution.py:33
  187.3 18.0 %all-to-all-start.2 = ((bf16[4,256,512]{1,2,0:T(8,128)(2,1)}), bf16[4,256,512]{1,2,0:T(8,128)(2,1)S(1)}, u32[]{:S(2)}, u32[]{:S(2)}) async-start(bf16[4,256,512]{1,2,0:T(8,128)(2,1)} %broadcast_in_dim.116), calls=%async_computation.2 | async-start | bytes 2097152 | tf_op jit(solution)/shard_map/all_to_all | solution.py:40
  251.5 21.2 %copy-start.1 = (bf16[256,2048]{1,0:T(8,128)(2,1)S(1)}, bf16[256,2048]{1,0:T(8,128)(2,1)}, u32[]{:S(2)}) copy-start(bf16[256,2048]{1,0:T(8,128)(2,1)} %param.11) | copy-start | bytes 3145732
  (8 other events, 27.6 us)
Sparse Core Ops, SparseCore 0:
  40.6 91.9 all-gather.4
  135.6 85.7 all-gather.6

commit v3 on v2

--- a/solution.py
+++ b/solution.py
@@ -79,11 +79,14 @@
     heads_here = quarter // HEAD
     hidden_here = gate_weight.shape[1]
 
-    out_t = gather_rows(out_weight.T, n_pairs)
-    rest = gather_rows(jnp.concatenate([gate_weight, up_weight, down_weight.T], axis=1), n_pairs)
-    gate_full = rest[:, :hidden_here]
-    up_full = rest[:, hidden_here:2 * hidden_here]
-    down_t = rest[:, 2 * hidden_here:]
+    quarter_cols = 2 * hidden_here
+    full = gather_rows(
+        jnp.concatenate([gate_weight, up_weight, out_weight.T, down_weight.T], axis=1), n_pairs
+    )
+    gate_full = full[:, :hidden_here]
+    up_full = full[:, hidden_here:quarter_cols]
+    out_t = full[:, quarter_cols:quarter_cols + quarter]
+    down_t = full[:, quarter_cols + quarter:]
 
     live_mask = slot_kind > 0
     first_mask = slot_kind == 2

time: 281 us -> 265 us (0.943)
  the two profiles are of different devices: /device:TPU:16 before, /device:TPU:8 now
where the time goes in v3:
time: 265 us; the launch traced here: 264 us
  waiting for transfers between devices  81.1 us (31%)
  matrix products  45.9 us (17%)
  starting transfers between devices  35.8 us (14%)
  other arithmetic  32.4 us (12%)
  blocking collectives  29.2 us (11%)
  local copies, waits for them, and re-layouts  25.2 us (10%)
  between operations  14 us (5%)
    ppermute x7, waiting for transfers between devices, carried_in(): got = lax.ppermute(packed, REQ, [(i, i + hop) for i in range(count - hop)])  45.9 us
    ppermute x7, starting transfers between devices, carried_in(): got = lax.ppermute(packed, REQ, [(i, i + hop) for i in range(count - hop)])  24.9 us
    dot_general x1, matrix products, on_device(): jnp.einsum('ctnk,ctsnk->ctsn', q4, decay_pairs * k4[:, None], precision=TOP)  17.8 us
    all_to_all x1, blocking collectives, mlp_sum(): got = lax.all_to_all(blocks, 'mlp', 0, 0)  16.1 us
    all_to_all x1, waiting for transfers between devices, mlp_sum(): got = lax.all_to_all(blocks, 'mlp', 0, 0)  15.2 us
    all_to_all x1, waiting for transfers between devices, mlp_gather(): got = lax.all_to_all(sent, 'mlp', 0, 0)  14.1 us
    all_to_all x1, blocking collectives, gather_rows(): over_cores = lax.all_to_all(sent, 'rc', 0, 0)  13.1 us
    mul x1, other arithmetic, on_device(): decay_pairs * k4[:, None]  11.1 us
  transfers between devices with their start and end apart: 11, of which 7 were waited for; matrix products, arithmetic and copies ran while one was open for 30% of the time, Pallas kernels for 0%

profile of v3, /device:TPU:8, one launch (start us, length us, event | category | flops | bytes accessed | tf_op | source)
XLA Modules:
  0.0 263.6 jit_solution(968375071416968240)
XLA Ops:
  17.2 4.6 %fusion.19 = f32[4,128,1,128]{3,2,1,0:T(1,128)S(1)} fusion(f32[8,4,128,1]{0,3,2,1:T(1,128)S(1)} %copy-done.14, f32[8,4,128,128]{3,2,1,0:T(8,128)S(1)} %fusion.61), kind=kOutput, calls=%fused_computation.23 | convolution fusion | flops 6291456 | bytes 2375680 | tf_op jit(solution)/shard_map/chk,chkv->hkv/dot_general | solution.py:117
  24.5 13.3 %collective-permute-done = f32[4,129,128]{2,1,0:T(8,128)} collective-permute-done((f32[4,129,128]{2,1,0:T(8,128)}, f32[4,129,128]{2,1,0:T(8,128)}, u32[]{:S(2)}, u32[]{:S(2)}) %collective-permute-start) | collective-permute-done | bytes 264224 | tf_op jit(solution)/shard_map/ppermute | solution.py:23
  42.3 9.5 %collective-permute-done.1 = f32[4,129,128]{2,1,0:T(8,128)S(1)} collective-permute-done((f32[4,129,128]{2,1,0:T(8,128)}, f32[4,129,128]{2,1,0:T(8,128)S(1)}, u32[]{:S(2)}, u32[]{:S(2)}) %collective-permute-start.1) | collective-permute-done | bytes 264224 | tf_op jit(solution)/shard_map/ppermute | solution.py:23
  55.6 12.0 %collective-permute-done.2 = f32[4,129,128]{2,1,0:T(8,128)} collective-permute-done((f32[4,129,128]{2,1,0:T(8,128)S(1)}, f32[4,129,128]{2,1,0:T(8,128)}, u32[]{:S(2)}, u32[]{:S(2)}) %collective-permute-start.2) | collective-permute-done | bytes 264224 | tf_op jit(solution)/shard_map/ppermute | solution.py:23
  69.5 5.3 %collective-permute-start.3 = (f32[4,129,128]{2,1,0:T(8,128)S(1)}, f32[4,129,128]{2,1,0:T(8,128)}, u32[]{:S(2)}, u32[]{:S(2)}) collective-permute-start(f32[4,129,128]{2,1,0:T(8,128)S(1)} %maximum_select_fusion.2), channel_id=1, source_target_pairs={{0,32},{4,36},{8,40},{12,44},{16,48},{20,52},{24,56},{28,60},{32,6... | collective-permute-start | bytes 792584 | tf_op jit(solution)/shard_map/ppermute | solution.py:23
  74.8 2.2 copy.109
  77.0 11.1 %collective-permute-done.3 = f32[4,129,128]{2,1,0:T(8,128)} collective-permute-done((f32[4,129,128]{2,1,0:T(8,128)S(1)}, f32[4,129,128]{2,1,0:T(8,128)}, u32[]{:S(2)}, u32[]{:S(2)}) %collective-permute-start.3) | collective-permute-done | bytes 264224 | tf_op jit(solution)/shard_map/ppermute | solution.py:23
  90.0 3.3 %collective-permute-start.4 = (f32[4,129,128]{2,1,0:T(8,128)S(1)}, f32[4,129,128]{2,1,0:T(8,128)}, u32[]{:S(2)}, u32[]{:S(2)}) collective-permute-start(f32[4,129,128]{2,1,0:T(8,128)S(1)} %maximum_select_fusion.3), channel_id=1, source_target_pairs={{0,64},{4,68},{8,72},{12,76},{16,80},{20,84},{24,88},{28,92},{32,9... | collective-permute-start | bytes 792584 | tf_op jit(solution)/shard_map/ppermute | solution.py:23
  93.3 11.1 %select_multiply_fusion = f32[8,32,32,4,128]{4,3,2,1,0:T(4,128)} fusion(f32[8,32,4,128]{3,2,1,0:T(4,128)} %copy-done.4, f32[8,32,4,128]{3,2,1,0:T(4,128)S(1)} %copy-done.3, pred[32,32]{1,0:T(8,128)(4,1)S(1)} %iota_compare_fusion), kind=kLoop, calls=%fused_computation.2 | loop fusion | flops 16777216 | bytes 17826816 | tf_op jit(solution)/shard_map/mul | solution.py:125
  104.4 2.7 %reshape.131 = bf16[8,32,4,128,1]{3,4,2,1,0:T(2,128)(2,1)} reshape(bf16[256,512]{1,0:T(8,128)(2,1)} %param.12) | data formatting | bytes 524288 | tf_op jit(solution)/shard_map/reshape;reshape | solution.py:107
  109.0 8.5 %collective-permute-start.5 = (f32[4,129,128]{2,1,0:T(8,128)S(1)}, f32[4,129,128]{2,1,0:T(8,128)}, u32[]{:S(2)}, u32[]{:S(2)}) collective-permute-start(f32[4,129,128]{2,1,0:T(8,128)S(1)} %maximum_select_fusion.4), channel_id=1, source_target_pairs={{0,128},{4,132},{8,136},{12,140},{16,144},{20,148},{24,152},{28,15... | collective-permute-start | bytes 792584 | tf_op jit(solution)/shard_map/ppermute | solution.py:23
  117.5 17.8 %fusion = f32[8,32,4,1,32]{4,3,2,1,0:T(1,128)} fusion(bf16[8,32,4,128,1]{3,4,2,1,0:T(2,128)(2,1)} %reshape.131, f32[8,32,32,4,128]{4,3,2,1,0:T(4,128)} %select_multiply_fusion), kind=kOutput, calls=%fused_computation | convolution fusion | flops 50331648 | bytes 17170432 | tf_op jit(solution)/shard_map/ctnk,ctsnk->ctsn/dot_general | solution.py:125
  141.8 7.2 %fusion.22 = f32[8,4,128,128]{3,0,2,1:T(8,128)} fusion(f32[8,4,128,128]{3,2,1,0:T(8,128)S(1)} %fusion.61, f32[8,4,128]{0,2,1:T(8,128)} %copy.120, f32[8,4,128]{0,2,1:T(8,128)} %copy.119, pred[8,8]{1,0:T(8,128)(4,1)S(1)} %iota_compare_fusion.1), kind=kOutput, calls=%fused_computation.26 | convolution fusion | flops 50429952 | bytes 4227136 | tf_op jit(solution)/shard_map/cdhk,dhkv->chkv/dot_general | solution.py:131
  156.8 5.9 %collective-permute-done.7 = f32[4,129,128]{2,1,0:T(8,128)S(1)} collective-permute-done((f32[4,129,128]{2,1,0:T(8,128)S(1)}, f32[4,129,128]{2,1,0:T(8,128)S(1)}, u32[]{:S(2)}, u32[]{:S(2)}) %collective-permute-start.7) | collective-permute-done | bytes 264224 | tf_op jit(solution)/shard_map/ppermute | solution.py:26
  164.8 4.4 %broadcast_in_dim.109 = bf16[2,64,16,2816]{3,2,1,0:T(8,128)(2,1)S(1)} broadcast(bf16[64,16,2816]{2,1,0:T(8,128)(2,1)} %bitcast.90), dimensions={1,2,3} | broadcast | bytes 17301504 | tf_op jit(solution)/shard_map/broadcast_in_dim | solution.py:46
  169.2 13.1 %all_to_all.20 = bf16[2,64,16,2816]{3,2,1,0:T(8,128)(2,1)S(1)} all-to-all(bf16[2,64,16,2816]{3,2,1,0:T(8,128)(2,1)S(1)} %broadcast_in_dim.109), channel_id=1, replica_groups=mesh['rp'=64,'rc'=2,'mlp'=4] {'rc'}, dimensions={0} | all-to-all | bytes 23068672 | tf_op jit(solution)/shard_map/all_to_all | solution.py:47
  182.7 4.0 %copy-done.1 = bf16[2,64,16,2816]{3,2,1,0:T(8,128)(2,1)} copy-done((bf16[2,64,16,2816]{3,2,1,0:T(8,128)(2,1)}, bf16[2,64,16,2816]{3,2,1,0:T(8,128)(2,1)S(1)}, u32[]{:S(2)}) %copy-start.1) | copy-done | bytes 11534360
  189.1 5.1 %all-to-all-start.1 = ((bf16[4,256,512]{1,2,0:T(8,128)(2,1)}), bf16[4,256,512]{1,2,0:T(8,128)(2,1)S(1)}, u32[]{:S(2)}, u32[]{:S(2)}) async-start(bf16[4,256,512]{1,2,0:T(8,128)(2,1)} %bitcast.29), calls=%async_computation.1 | async-start | bytes 2097152 | tf_op jit(solution)/shard_map/all_to_all | solution.py:33
  194.3 15.2 %all-to-all-done.1 = bf16[4,256,512]{1,2,0:T(8,128)(2,1)S(1)} async-done(((bf16[4,256,512]{1,2,0:T(8,128)(2,1)}), bf16[4,256,512]{1,2,0:T(8,128)(2,1)S(1)}, u32[]{:S(2)}, u32[]{:S(2)}) %all-to-all-start.1) | async-done | bytes 1048608 | tf_op jit(solution)/shard_map/all_to_all | solution.py:33
  210.8 3.8 %all-to-all-start.2 = ((bf16[4,256,512]{1,2,0:T(8,128)(2,1)}), bf16[4,256,512]{1,2,0:T(8,128)(2,1)S(1)}, u32[]{:S(2)}, u32[]{:S(2)}) async-start(bf16[4,256,512]{1,2,0:T(8,128)(2,1)} %broadcast_in_dim.110), calls=%async_computation.2 | async-start | bytes 2097152 | tf_op jit(solution)/shard_map/all_to_all | solution.py:40
  214.8 14.1 %all-to-all-done.2 = bf16[4,256,512]{1,2,0:T(8,128)(2,1)S(1)} async-done(((bf16[4,256,512]{1,2,0:T(8,128)(2,1)}), bf16[4,256,512]{1,2,0:T(8,128)(2,1)S(1)}, u32[]{:S(2)}, u32[]{:S(2)}) %all-to-all-start.2) | async-done | bytes 1048608 | tf_op jit(solution)/shard_map/all_to_all | solution.py:40
  229.8 3.8 %fusion.6 = f32[256,768]{1,0:T(8,128)} fusion(bf16[256,2048]{0,1:T(8,128)(2,1)S(1)} %bitcast.97, bf16[2048,2816]{1,0:T(8,128)(2,1)} %bitcast.87), kind=kOutput, calls=%fused_computation.7 | convolution fusion | flops 805306368 | bytes 4980736 | tf_op jit(solution)/shard_map/dot_general | solution.py:155
  233.6 5.3 %fusion.8 = bf16[256,2048]{1,0:T(8,128)(2,1)S(1)} fusion(bf16[2048,2816]{1,0:T(8,128)(2,1)} %bitcast.88, bf16[256,2048]{0,1:T(8,128)(2,1)S(1)} %bitcast.98, f32[256,768]{1,0:T(8,128)} %fusion.6), kind=kOutput, calls=%fused_computation.10 | convolution fusion | flops 1612316672 | bytes 9175040 | tf_op jit(solution)/shard_map/dot_general | solution.py:158
  239.6 16.1 %all_to_all.21 = bf16[4,256,512]{1,2,0:T(8,128)(2,1)S(1)} all-to-all(bf16[4,256,512]{1,2,0:T(8,128)(2,1)S(1)} %bitcast.96), channel_id=1, replica_groups=mesh['rp'=64,'rc'=2,'mlp'=4] {'mlp'}, dimensions={0} | all-to-all | bytes 2097152 | tf_op jit(solution)/shard_map/all_to_all | solution.py:33
  (120 shorter events, 50.3 us)
Async XLA Ops:
  6.5 187.6 %copy-start = (bf16[256,2048]{1,0:T(8,128)(2,1)S(1)}, bf16[256,2048]{1,0:T(8,128)(2,1)}, u32[]{:S(2)}) copy-start(bf16[256,2048]{1,0:T(8,128)(2,1)} %param.11) | copy-start | bytes 3145732
  6.5 158.2 %all-gather.3.cloned.1.call-start = ((), (), s32[]{:S(2)}) async-start(), calls=%async_computation.4 | async-start | bytes 5857280 | tf_op jit(solution)/shard_map/all_gather | solution.py:45
  22.5 15.3 %collective-permute-start = (f32[4,129,128]{2,1,0:T(8,128)}, f32[4,129,128]{2,1,0:T(8,128)}, u32[]{:S(2)}, u32[]{:S(2)}) collective-permute-start(f32[4,129,128]{2,1,0:T(8,128)} %pad_maximum_fusion), channel_id=1, source_target_pairs={{0,4},{4,8},{8,12},{12,16},{16,20},{20,24},{24,28},{28,32},{32,36}... | collective-permute-start | bytes 792584 | tf_op jit(solution)/shard_map/ppermute | solution.py:23
  40.4 11.4 %collective-permute-start.1 = (f32[4,129,128]{2,1,0:T(8,128)}, f32[4,129,128]{2,1,0:T(8,128)S(1)}, u32[]{:S(2)}, u32[]{:S(2)}) collective-permute-start(f32[4,129,128]{2,1,0:T(8,128)} %maximum_select_fusion), channel_id=1, source_target_pairs={{0,8},{4,12},{8,16},{12,20},{16,24},{20,28},{24,32},{28,36},{32,40... | collective-permute-start | bytes 792584 | tf_op jit(solution)/shard_map/ppermute | solution.py:23
  53.7 15.7 %copy-start.8 = (f32[4,129,128]{2,1,0:T(8,128)}, f32[4,129,128]{2,1,0:T(8,128)S(1)}, u32[]{:S(2)}) copy-start(f32[4,129,128]{2,1,0:T(8,128)S(1)} %maximum_select_fusion.1) | copy-start | bytes 792580
  53.7 13.9 %collective-permute-start.2 = (f32[4,129,128]{2,1,0:T(8,128)S(1)}, f32[4,129,128]{2,1,0:T(8,128)}, u32[]{:S(2)}, u32[]{:S(2)}) collective-permute-start(f32[4,129,128]{2,1,0:T(8,128)S(1)} %maximum_select_fusion.1), channel_id=1, source_target_pairs={{0,16},{4,20},{8,24},{12,28},{16,32},{20,36},{24,40},{28,44},{32,4... | collective-permute-start | bytes 792584 | tf_op jit(solution)/shard_map/ppermute | solution.py:23
  69.5 20.5 %copy-start.7 = (f32[4,129,128]{2,1,0:T(8,128)}, f32[4,129,128]{2,1,0:T(8,128)S(1)}, u32[]{:S(2)}) copy-start(f32[4,129,128]{2,1,0:T(8,128)S(1)} %maximum_select_fusion.2) | copy-start | bytes 792580
  69.5 18.7 %collective-permute-start.3 = (f32[4,129,128]{2,1,0:T(8,128)S(1)}, f32[4,129,128]{2,1,0:T(8,128)}, u32[]{:S(2)}, u32[]{:S(2)}) collective-permute-start(f32[4,129,128]{2,1,0:T(8,128)S(1)} %maximum_select_fusion.2), channel_id=1, source_target_pairs={{0,32},{4,36},{8,40},{12,44},{16,48},{20,52},{24,56},{28,60},{32,6... | collective-permute-start | bytes 792584 | tf_op jit(solution)/shard_map/ppermute | solution.py:23
  77.0 16.3 %copy-start.3 = (f32[8,32,4,128]{3,2,1,0:T(4,128)S(1)}, f32[8,32,4,128]{3,2,1,0:T(4,128)}, u32[]{:S(2)}) copy-start(f32[8,32,4,128]{3,2,1,0:T(4,128)} %copy.109) | copy-start | bytes 1572868
  90.0 17.8 %copy-start.6 = (f32[4,129,128]{2,1,0:T(8,128)}, f32[4,129,128]{2,1,0:T(8,128)S(1)}, u32[]{:S(2)}) copy-start(f32[4,129,128]{2,1,0:T(8,128)S(1)} %maximum_select_fusion.3) | copy-start | bytes 792580
  90.0 17.1 %collective-permute-start.4 = (f32[4,129,128]{2,1,0:T(8,128)S(1)}, f32[4,129,128]{2,1,0:T(8,128)}, u32[]{:S(2)}, u32[]{:S(2)}) collective-permute-start(f32[4,129,128]{2,1,0:T(8,128)S(1)} %maximum_select_fusion.3), channel_id=1, source_target_pairs={{0,64},{4,68},{8,72},{12,76},{16,80},{20,84},{24,88},{28,92},{32,9... | collective-permute-start | bytes 792584 | tf_op jit(solution)/shard_map/ppermute | solution.py:23
  109.0 28.8 %copy-start.5 = (f32[4,129,128]{2,1,0:T(8,128)}, f32[4,129,128]{2,1,0:T(8,128)S(1)}, u32[]{:S(2)}) copy-start(f32[4,129,128]{2,1,0:T(8,128)S(1)} %maximum_select_fusion.4) | copy-start | bytes 792580
  109.0 28.0 %collective-permute-start.5 = (f32[4,129,128]{2,1,0:T(8,128)S(1)}, f32[4,129,128]{2,1,0:T(8,128)}, u32[]{:S(2)}, u32[]{:S(2)}) collective-permute-start(f32[4,129,128]{2,1,0:T(8,128)S(1)} %maximum_select_fusion.4), channel_id=1, source_target_pairs={{0,128},{4,132},{8,136},{12,140},{16,144},{20,148},{24,152},{28,15... | collective-permute-start | bytes 792584 | tf_op jit(solution)/shard_map/ppermute | solution.py:23
  139.8 10.9 %collective-permute-start.6 = (f32[4,129,128]{2,1,0:T(8,128)S(1)}, f32[4,129,128]{2,1,0:T(8,128)}, u32[]{:S(2)}, u32[]{:S(2)}) collective-permute-start(f32[4,129,128]{2,1,0:T(8,128)S(1)} %maximum_select_fusion.5), channel_id=1, source_target_pairs={{0,256},{4,260},{8,264},{12,268},{16,272},{20,276},{24,280},{28,28... | collective-permute-start | bytes 792584 | tf_op jit(solution)/shard_map/ppermute | solution.py:23
  149.1 5.6 %copy-start.10 = (f32[8,4,128,128]{3,0,2,1:T(8,128)S(1)}, f32[8,4,128,128]{3,0,2,1:T(8,128)}, u32[]{:S(2)}) copy-start(f32[8,4,128,128]{3,0,2,1:T(8,128)} %fusion.22) | copy-start | bytes 6291460
  149.1 5.6 %copy-start.12 = (f32[8,32,4,128]{3,0,1,2:T(8,128)S(1)}, f32[8,32,4,128]{3,0,1,2:T(8,128)}, u32[]{:S(2)}) copy-start(f32[8,32,4,128]{3,0,1,2:T(8,128)} %get-tuple-element.6) | copy-start | bytes 1572868
  152.5 10.2 %copy-start.11 = (f32[8,32,4,128]{3,0,1,2:T(8,128)S(1)}, f32[8,32,4,128]{3,0,1,2:T(8,128)}, u32[]{:S(2)}) copy-start(f32[8,32,4,128]{3,0,1,2:T(8,128)} %get-tuple-element.5) | copy-start | bytes 1572868
  152.6 10.1 %collective-permute-start.7 = (f32[4,129,128]{2,1,0:T(8,128)S(1)}, f32[4,129,128]{2,1,0:T(8,128)S(1)}, u32[]{:S(2)}, u32[]{:S(2)}) collective-permute-start(f32[4,129,128]{2,1,0:T(8,128)S(1)} %maximum_select_fusion.6), channel_id=1, source_target_pairs={{0,4},{4,8},{8,12},{12,16},{16,20},{20,24},{24,28},{28,32},{32,36}... | collective-permute-start | bytes 792584 | tf_op jit(solution)/shard_map/ppermute | solution.py:26
  169.2 17.5 %copy-start.15 = (f32[8,32,4,128]{3,2,1,0:T(4,128)S(1)}, f32[8,32,4,128]{3,2,1,0:T(4,128)}, u32[]{:S(2)}) copy-start(f32[8,32,4,128]{3,2,1,0:T(4,128)} %copy.127) | copy-start | bytes 1572868
  169.2 17.5 %copy-start.17 = (f32[512]{0:T(512)S(1)}, f32[512]{0:T(512)}, u32[]{:S(2)}) copy-start(f32[512]{0:T(512)} %param.16) | copy-start | bytes 6148
  182.3 4.3 %copy-start.1 = (bf16[2,64,16,2816]{3,2,1,0:T(8,128)(2,1)}, bf16[2,64,16,2816]{3,2,1,0:T(8,128)(2,1)S(1)}, u32[]{:S(2)}) copy-start(bf16[2,64,16,2816]{3,2,1,0:T(8,128)(2,1)S(1)} %all_to_all.20) | copy-start | bytes 34603012
  189.1 20.5 %all-to-all-start.1 = ((bf16[4,256,512]{1,2,0:T(8,128)(2,1)}), bf16[4,256,512]{1,2,0:T(8,128)(2,1)S(1)}, u32[]{:S(2)}, u32[]{:S(2)}) async-start(bf16[4,256,512]{1,2,0:T(8,128)(2,1)} %bitcast.29), calls=%async_computation.1 | async-start | bytes 2097152 | tf_op jit(solution)/shard_map/all_to_all | solution.py:33
  209.7 4.9 %copy-start.16 = (f32[2048]{0:T(1024)S(1)}, f32[2048]{0:T(1024)}, u32[]{:S(2)}) copy-start(f32[2048]{0:T(1024)} %param.18) | copy-start | bytes 24580
  210.8 18.0 %all-to-all-start.2 = ((bf16[4,256,512]{1,2,0:T(8,128)(2,1)}), bf16[4,256,512]{1,2,0:T(8,128)(2,1)S(1)}, u32[]{:S(2)}, u32[]{:S(2)}) async-start(bf16[4,256,512]{1,2,0:T(8,128)(2,1)} %broadcast_in_dim.110), calls=%async_computation.2 | async-start | bytes 2097152 | tf_op jit(solution)/shard_map/all_to_all | solution.py:40
  (5 other events, 13.1 us)
Sparse Core Ops, SparseCore 0:
  10.4 120.2 all-gather.2

commit v4 on v3

--- a/solution.py
+++ b/solution.py
@@ -32,13 +32,6 @@
     blocks = parts.reshape(rows, n_mlp, width // n_mlp).transpose(1, 0, 2)
     got = lax.all_to_all(blocks, "mlp", 0, 0)
     return jnp.sum(got.astype(jnp.float32), axis=0)
-
-
-def mlp_gather(cols, n_mlp):
-    rows, width = cols.shape
-    sent = jnp.broadcast_to(cols[None], (n_mlp, rows, width))
-    got = lax.all_to_all(sent, "mlp", 0, 0)
-    return got.transpose(1, 0, 2).reshape(rows, n_mlp * width)
 
 
 def gather_rows(piece, n_pairs):
@@ -141,11 +134,13 @@
     partial_rows = to_natural(lax.dot_general(
         head_normed, out_t, (((1,), (1,)), ((), ())), preferred_element_type=jnp.float32
     ).astype(jnp.bfloat16), n_pairs)
-    mixed_cols = mlp_sum(partial_rows, n_mlp)
+    every = lax.all_to_all(
+        jnp.broadcast_to(partial_rows[None], (n_mlp,) + partial_rows.shape), "mlp", 0, 0
+    )
+    mixed = jnp.sum(every.astype(jnp.float32), axis=0)
+    stream = (residual.astype(jnp.float32) + mixed).astype(jnp.bfloat16)
     my_cols = lax.axis_index("mlp") * quarter
-    own_res = lax.dynamic_slice_in_dim(residual, my_cols, quarter, 1).astype(jnp.float32)
-    stream_cols = (own_res + mixed_cols).astype(jnp.bfloat16)
-    stream = mlp_gather(stream_cols, n_mlp)
+    stream_cols = lax.dynamic_slice_in_dim(stream, my_cols, quarter, 1)
 
     rows_f = stream.astype(jnp.float32)
     ffn_in = (

time: 265 us -> 273 us (1.030)
  the two profiles are of different devices: /device:TPU:8 before, /device:TPU:48 now
where the time goes in v4:
time: 273 us; the launch traced here: 271 us
  waiting for transfers between devices  80.4 us (29%)
  blocking collectives  66.1 us (24%)
  matrix products  43.8 us (16%)
  other arithmetic  25.5 us (9%)
  starting transfers between devices  23.7 us (9%)
  local copies, waits for them, and re-layouts  18 us (7%)
  between operations  14 us (5%)
    ppermute x7, waiting for transfers between devices, carried_in(): got = lax.ppermute(packed, REQ, [(i, i + hop) for i in range(count - hop)])  60.3 us
    all_to_all x1, blocking collectives, on_device(): lax.all_to_all(jnp.broadcast_to(partial_rows[None], (n_mlp,) + partial_ro...  53.1 us
    ppermute x7, starting transfers between devices, carried_in(): got = lax.ppermute(packed, REQ, [(i, i + hop) for i in range(count - hop)])  18.1 us
    dot_general x1, matrix products, on_device(): jnp.einsum('ctnk,ctsnk->ctsn', q4, decay_pairs * k4[:, None], precision=TOP)  17.2 us
    all_to_all x1, waiting for transfers between devices, mlp_sum(): got = lax.all_to_all(blocks, 'mlp', 0, 0)  14.2 us
    all_to_all x1, blocking collectives, gather_rows(): over_cores = lax.all_to_all(sent, 'rc', 0, 0)  13 us
    mul x1, other arithmetic, on_device(): decay_pairs * k4[:, None]  11.1 us
    dot_general x1, matrix products, on_device(): local_in = jnp.einsum('cdhk,dhkv->chkv', weights, span_state, precision=TOP)  7.16 us
  transfers between devices with their start and end apart: 10, of which 8 were waited for; matrix products, arithmetic and copies ran while one was open for 22% of the time, Pallas kernels for 0%

profile of v4, /device:TPU:48, one launch (start us, length us, event | category | flops | bytes accessed | tf_op | source)
XLA Modules:
  0.0 271.5 jit_solution(4528230979458169805)
XLA Ops:
  14.8 4.6 %fusion.22 = f32[4,128,1,128]{3,2,1,0:T(1,128)S(1)} fusion(f32[8,4,128,1]{0,3,2,1:T(1,128)S(1)} %copy.229, f32[8,4,128,128]{3,2,1,0:T(8,128)S(1)} %fusion.63), kind=kOutput, calls=%fused_computation.27 | convolution fusion | flops 6291456 | bytes 2375680 | tf_op jit(solution)/shard_map/chk,chkv->hkv/dot_general | solution.py:110
  21.4 13.4 %collective-permute-done = f32[4,129,128]{2,1,0:T(8,128)S(1)} collective-permute-done((f32[4,129,128]{2,1,0:T(8,128)S(1)}, f32[4,129,128]{2,1,0:T(8,128)S(1)}, u32[]{:S(2)}, u32[]{:S(2)}) %collective-permute-start) | collective-permute-done | bytes 264224 | tf_op jit(solution)/shard_map/ppermute | solution.py:23
  35.0 1.9 collective-permute-start.1
  36.9 9.0 %collective-permute-done.1 = f32[4,129,128]{2,1,0:T(8,128)S(1)} collective-permute-done((f32[4,129,128]{2,1,0:T(8,128)S(1)}, f32[4,129,128]{2,1,0:T(8,128)S(1)}, u32[]{:S(2)}, u32[]{:S(2)}) %collective-permute-start.1) | collective-permute-done | bytes 264224 | tf_op jit(solution)/shard_map/ppermute | solution.py:23
  48.1 11.8 %collective-permute-done.2 = f32[4,129,128]{2,1,0:T(8,128)S(1)} collective-permute-done((f32[4,129,128]{2,1,0:T(8,128)S(1)}, f32[4,129,128]{2,1,0:T(8,128)S(1)}, u32[]{:S(2)}, u32[]{:S(2)}) %collective-permute-start.2) | collective-permute-done | bytes 264224 | tf_op jit(solution)/shard_map/ppermute | solution.py:23
  60.1 6.6 %collective-permute-start.3 = (f32[4,129,128]{2,1,0:T(8,128)S(1)}, f32[4,129,128]{2,1,0:T(8,128)}, u32[]{:S(2)}, u32[]{:S(2)}) collective-permute-start(f32[4,129,128]{2,1,0:T(8,128)S(1)} %maximum_select_fusion.2), channel_id=1, source_target_pairs={{0,32},{4,36},{8,40},{12,44},{16,48},{20,52},{24,56},{28,60},{32,6... | collective-permute-start | bytes 792584 | tf_op jit(solution)/shard_map/ppermute | solution.py:23
  67.2 13.0 %collective-permute-done.3 = f32[4,129,128]{2,1,0:T(8,128)} collective-permute-done((f32[4,129,128]{2,1,0:T(8,128)S(1)}, f32[4,129,128]{2,1,0:T(8,128)}, u32[]{:S(2)}, u32[]{:S(2)}) %collective-permute-start.3) | collective-permute-done | bytes 264224 | tf_op jit(solution)/shard_map/ppermute | solution.py:23
  82.0 2.6 collective-permute-start.4
  84.5 11.1 %select_multiply_fusion = f32[8,32,32,4,128]{4,3,2,1,0:T(4,128)} fusion(f32[8,32,4,128]{3,2,1,0:T(4,128)} %copy-done.1, f32[8,32,4,128]{3,2,1,0:T(4,128)S(1)} %copy.199, pred[32,32]{1,0:T(8,128)(4,1)S(1)} %iota_compare_fusion), kind=kLoop, calls=%fused_computation.2 | loop fusion | flops 16777216 | bytes 17826816 | tf_op jit(solution)/shard_map/mul | solution.py:118
  99.8 17.2 %fusion = f32[8,32,4,1,32]{4,3,2,1,0:T(1,128)S(1)} fusion(bf16[8,32,4,128,1]{3,4,2,1,0:T(2,128)(2,1)} %reshape.119, f32[8,32,32,4,128]{4,3,2,1,0:T(4,128)} %select_multiply_fusion), kind=kOutput, calls=%fused_computation | convolution fusion | flops 50331648 | bytes 17170432 | tf_op jit(solution)/shard_map/ctnk,ctsnk->ctsn/dot_general | solution.py:118
  118.0 2.8 %collective-permute-done.5 = f32[4,129,128]{2,1,0:T(8,128)S(1)} collective-permute-done((f32[4,129,128]{2,1,0:T(8,128)S(1)}, f32[4,129,128]{2,1,0:T(8,128)S(1)}, u32[]{:S(2)}, u32[]{:S(2)}) %collective-permute-start.5) | collective-permute-done | bytes 264224 | tf_op jit(solution)/shard_map/ppermute | solution.py:23
  122.7 7.2 %fusion.25 = f32[8,4,128,128]{3,0,2,1:T(8,128)} fusion(f32[8,4,128,128]{3,2,1,0:T(8,128)S(1)} %fusion.63, f32[8,4,128]{0,2,1:T(8,128)} %copy.208, f32[8,4,128]{0,2,1:T(8,128)S(1)} %copy.207, pred[8,8]{1,0:T(8,128)(4,1)S(1)} %iota_compare_fusion.1), kind=kOutput, calls=%fused_computation.30 | convolution fusion | flops 50429952 | bytes 4227136 | tf_op jit(solution)/shard_map/cdhk,dhkv->chkv/dot_general | solution.py:124
  130.3 10.2 %collective-permute-done.6 = f32[4,129,128]{2,1,0:T(8,128)} collective-permute-done((f32[4,129,128]{2,1,0:T(8,128)S(1)}, f32[4,129,128]{2,1,0:T(8,128)}, u32[]{:S(2)}, u32[]{:S(2)}) %collective-permute-start.6) | collective-permute-done | bytes 264224 | tf_op jit(solution)/shard_map/ppermute | solution.py:23
  142.3 2.1 collective-permute-start.7
  144.4 2.2 fusion.39
  146.6 5.9 %collective-permute-done.7 = f32[4,129,128]{2,1,0:T(8,128)S(1)} collective-permute-done((f32[4,129,128]{2,1,0:T(8,128)S(1)}, f32[4,129,128]{2,1,0:T(8,128)S(1)}, u32[]{:S(2)}, u32[]{:S(2)}) %collective-permute-start.7) | collective-permute-done | bytes 264224 | tf_op jit(solution)/shard_map/ppermute | solution.py:26
  153.7 4.4 %broadcast_in_dim.110 = bf16[2,64,16,2816]{3,2,1,0:T(8,128)(2,1)S(1)} broadcast(bf16[64,16,2816]{2,1,0:T(8,128)(2,1)} %bitcast.85), dimensions={1,2,3} | broadcast | bytes 17301504 | tf_op jit(solution)/shard_map/broadcast_in_dim | solution.py:39
  158.2 13.0 %all_to_all.15 = bf16[2,64,16,2816]{3,2,1,0:T(8,128)(2,1)S(1)} all-to-all(bf16[2,64,16,2816]{3,2,1,0:T(8,128)(2,1)S(1)} %broadcast_in_dim.110), channel_id=1, replica_groups=mesh['rp'=64,'rc'=2,'mlp'=4] {'rc'}, dimensions={0} | all-to-all | bytes 23068672 | tf_op jit(solution)/shard_map/all_to_all | solution.py:40
  171.5 4.0 %copy-done = bf16[2,64,16,2816]{3,2,1,0:T(8,128)(2,1)} copy-done((bf16[2,64,16,2816]{3,2,1,0:T(8,128)(2,1)}, bf16[2,64,16,2816]{3,2,1,0:T(8,128)(2,1)S(1)}, u32[]{:S(2)}) %copy-start) | copy-done | bytes 11534360
  178.1 53.1 %all_to_all.16 = bf16[4,256,2048]{2,1,0:T(8,128)(2,1)S(1)} all-to-all(bf16[4,256,2048]{2,1,0:T(8,128)(2,1)S(1)} %broadcast_in_dim.112), channel_id=1, replica_groups=mesh['rp'=64,'rc'=2,'mlp'=4] {'mlp'}, dimensions={0} | all-to-all | bytes 8388608 | tf_op jit(solution)/shard_map/all_to_all | solution.py:137
  234.1 2.9 %fusion.6 = f32[256,768]{1,0:T(8,128)S(1)} fusion(bf16[256,2048]{0,1:T(8,128)(2,1)S(1)} %bitcast.93, bf16[2048,2816]{1,0:T(8,128)(2,1)} %bitcast.83), kind=kOutput, calls=%fused_computation.8 | convolution fusion | flops 805306368 | bytes 4980736 | tf_op jit(solution)/shard_map/dot_general | solution.py:150
  237.0 6.1 %fusion.8 = bf16[256,2048]{1,0:T(8,128)(2,1)} fusion(bf16[2048,2816]{1,0:T(8,128)(2,1)} %bitcast.84, bf16[256,2048]{0,1:T(8,128)(2,1)S(1)} %bitcast.94, f32[256,768]{1,0:T(8,128)S(1)} %fusion.6), kind=kOutput, calls=%fused_computation.13 | convolution fusion | flops 1612316672 | bytes 9175040 | tf_op jit(solution)/shard_map/dot_general | solution.py:153
  245.7 3.5 %all-to-all-start.2 = ((bf16[4,256,512]{1,2,0:T(8,128)(2,1)}), bf16[4,256,512]{1,2,0:T(8,128)(2,1)S(1)}, u32[]{:S(2)}, u32[]{:S(2)}) async-start(bf16[4,256,512]{1,2,0:T(8,128)(2,1)} %bitcast.35), calls=%async_computation.2 | async-start | bytes 2097152 | tf_op jit(solution)/shard_map/all_to_all | solution.py:33
  249.3 14.2 %all-to-all-done.2 = bf16[4,256,512]{1,2,0:T(8,128)(2,1)S(1)} async-done(((bf16[4,256,512]{1,2,0:T(8,128)(2,1)}), bf16[4,256,512]{1,2,0:T(8,128)(2,1)S(1)}, u32[]{:S(2)}, u32[]{:S(2)}) %all-to-all-start.2) | async-done | bytes 1048608 | tf_op jit(solution)/shard_map/all_to_all | solution.py:33
  (104 shorter events, 34.8 us)
Async XLA Ops:
  6.5 147.2 %all-gather.3.cloned.1.call-start = ((), (), s32[]{:S(2)}) async-start(), calls=%async_computation.3 | async-start | bytes 5857280 | tf_op jit(solution)/shard_map/all_gather | solution.py:38
  8.7 2.4 copy-start.9
  10.2 1.0 copy-start.11
  11.1 1.9 copy-start.1
  11.3 1.7 copy-start.3
  19.4 15.4 %collective-permute-start = (f32[4,129,128]{2,1,0:T(8,128)S(1)}, f32[4,129,128]{2,1,0:T(8,128)S(1)}, u32[]{:S(2)}, u32[]{:S(2)}) collective-permute-start(f32[4,129,128]{2,1,0:T(8,128)S(1)} %pad_maximum_fusion), channel_id=1, source_target_pairs={{0,4},{4,8},{8,12},{12,16},{16,20},{20,24},{24,28},{28,32},{32,36}... | collective-permute-start | bytes 792584 | tf_op jit(solution)/shard_map/ppermute | solution.py:23
  35.0 11.0 %collective-permute-start.1 = (f32[4,129,128]{2,1,0:T(8,128)S(1)}, f32[4,129,128]{2,1,0:T(8,128)S(1)}, u32[]{:S(2)}, u32[]{:S(2)}) collective-permute-start(f32[4,129,128]{2,1,0:T(8,128)S(1)} %maximum_select_fusion), channel_id=1, source_target_pairs={{0,8},{4,12},{8,16},{12,20},{16,24},{20,28},{24,32},{28,36},{32,40... | collective-permute-start | bytes 792584 | tf_op jit(solution)/shard_map/ppermute | solution.py:23
  46.1 13.9 %copy-start.2 = (f32[4,129,128]{2,1,0:T(8,128)}, f32[4,129,128]{2,1,0:T(8,128)S(1)}, u32[]{:S(2)}) copy-start(f32[4,129,128]{2,1,0:T(8,128)S(1)} %maximum_select_fusion.1) | copy-start | bytes 792580
  46.2 13.8 %collective-permute-start.2 = (f32[4,129,128]{2,1,0:T(8,128)S(1)}, f32[4,129,128]{2,1,0:T(8,128)S(1)}, u32[]{:S(2)}, u32[]{:S(2)}) collective-permute-start(f32[4,129,128]{2,1,0:T(8,128)S(1)} %maximum_select_fusion.1), channel_id=1, source_target_pairs={{0,16},{4,20},{8,24},{12,28},{16,32},{20,36},{24,40},{28,44},{32,4... | collective-permute-start | bytes 792584 | tf_op jit(solution)/shard_map/ppermute | solution.py:23
  60.1 20.0 %collective-permute-start.3 = (f32[4,129,128]{2,1,0:T(8,128)S(1)}, f32[4,129,128]{2,1,0:T(8,128)}, u32[]{:S(2)}, u32[]{:S(2)}) collective-permute-start(f32[4,129,128]{2,1,0:T(8,128)S(1)} %maximum_select_fusion.2), channel_id=1, source_target_pairs={{0,32},{4,36},{8,40},{12,44},{16,48},{20,52},{24,56},{28,60},{32,6... | collective-permute-start | bytes 792584 | tf_op jit(solution)/shard_map/ppermute | solution.py:23
  82.0 13.7 %copy-start.10 = (bf16[256,512]{1,0:T(8,128)(2,1)S(1)}, bf16[256,512]{1,0:T(8,128)(2,1)}, u32[]{:S(2)}) copy-start(bf16[256,512]{1,0:T(8,128)(2,1)} %param.12) | copy-start | bytes 786436
  82.0 14.5 %collective-permute-start.4 = (f32[4,129,128]{2,1,0:T(8,128)S(1)}, f32[4,129,128]{2,1,0:T(8,128)}, u32[]{:S(2)}, u32[]{:S(2)}) collective-permute-start(f32[4,129,128]{2,1,0:T(8,128)S(1)} %maximum_select_fusion.3), channel_id=1, source_target_pairs={{0,64},{4,68},{8,72},{12,76},{16,80},{20,84},{24,88},{28,92},{32,9... | collective-permute-start | bytes 792584 | tf_op jit(solution)/shard_map/ppermute | solution.py:23
  98.3 22.5 %collective-permute-start.5 = (f32[4,129,128]{2,1,0:T(8,128)S(1)}, f32[4,129,128]{2,1,0:T(8,128)S(1)}, u32[]{:S(2)}, u32[]{:S(2)}) collective-permute-start(f32[4,129,128]{2,1,0:T(8,128)S(1)} %maximum_select_fusion.4), channel_id=1, source_target_pairs={{0,128},{4,132},{8,136},{12,140},{16,144},{20,148},{24,152},{28,15... | collective-permute-start | bytes 792584 | tf_op jit(solution)/shard_map/ppermute | solution.py:23
  121.0 8.8 %copy-start.4 = (bf16[8,32,4,128]{3,2,1,0:T(4,128)(2,1)S(1)}, bf16[8,32,4,128]{3,2,1,0:T(4,128)(2,1)}, u32[]{:S(2)}) copy-start(bf16[8,32,4,128]{3,2,1,0:T(4,128)(2,1)} %copy-done.3) | copy-start | bytes 786436
  121.0 19.4 %collective-permute-start.6 = (f32[4,129,128]{2,1,0:T(8,128)S(1)}, f32[4,129,128]{2,1,0:T(8,128)}, u32[]{:S(2)}, u32[]{:S(2)}) collective-permute-start(f32[4,129,128]{2,1,0:T(8,128)S(1)} %maximum_select_fusion.5), channel_id=1, source_target_pairs={{0,256},{4,260},{8,264},{12,268},{16,272},{20,276},{24,280},{28,28... | collective-permute-start | bytes 792584 | tf_op jit(solution)/shard_map/ppermute | solution.py:23
  129.8 14.5 %copy-start.5 = (f32[8,4,128,128]{3,0,2,1:T(8,128)S(1)}, f32[8,4,128,128]{3,0,2,1:T(8,128)}, u32[]{:S(2)}) copy-start(f32[8,4,128,128]{3,0,2,1:T(8,128)} %fusion.25) | copy-start | bytes 6291460
  129.9 14.5 %copy-start.7 = (f32[8,32,4,128]{3,0,1,2:T(8,128)S(1)}, f32[8,32,4,128]{3,0,1,2:T(8,128)}, u32[]{:S(2)}) copy-start(f32[8,32,4,128]{3,0,1,2:T(8,128)} %get-tuple-element.8) | copy-start | bytes 1572868
  142.3 10.2 %copy-start.6 = (f32[8,32,4,128]{3,0,1,2:T(8,128)S(1)}, f32[8,32,4,128]{3,0,1,2:T(8,128)}, u32[]{:S(2)}) copy-start(f32[8,32,4,128]{3,0,1,2:T(8,128)} %get-tuple-element.7) | copy-start | bytes 1572868
  142.3 10.1 %collective-permute-start.7 = (f32[4,129,128]{2,1,0:T(8,128)S(1)}, f32[4,129,128]{2,1,0:T(8,128)S(1)}, u32[]{:S(2)}, u32[]{:S(2)}) collective-permute-start(f32[4,129,128]{2,1,0:T(8,128)S(1)} %maximum_select_fusion.6), channel_id=1, source_target_pairs={{0,4},{4,8},{8,12},{12,16},{16,20},{20,24},{24,28},{28,32},{32,36}... | collective-permute-start | bytes 792584 | tf_op jit(solution)/shard_map/ppermute | solution.py:26
  158.1 17.3 %copy-start.13 = (f32[512]{0:T(512)S(1)}, f32[512]{0:T(512)}, u32[]{:S(2)}) copy-start(f32[512]{0:T(512)} %param.16) | copy-start | bytes 6148
  171.2 4.3 %copy-start = (bf16[2,64,16,2816]{3,2,1,0:T(8,128)(2,1)}, bf16[2,64,16,2816]{3,2,1,0:T(8,128)(2,1)S(1)}, u32[]{:S(2)}) copy-start(bf16[2,64,16,2816]{3,2,1,0:T(8,128)(2,1)S(1)} %all_to_all.15) | copy-start | bytes 34603012
  231.2 1.2 copy-start.8
  232.4 0.7 copy-start.12
  245.7 17.7 %all-to-all-start.2 = ((bf16[4,256,512]{1,2,0:T(8,128)(2,1)}), bf16[4,256,512]{1,2,0:T(8,128)(2,1)S(1)}, u32[]{:S(2)}, u32[]{:S(2)}) async-start(bf16[4,256,512]{1,2,0:T(8,128)(2,1)} %bitcast.35), calls=%async_computation.2 | async-start | bytes 2097152 | tf_op jit(solution)/shard_map/all_to_all | solution.py:33
Sparse Core Ops, SparseCore 0:
  10.4 119.8 all-gather.2
